TPU v7x, 128 devices: a whole 4x4x4 slice. The times are simulated.
128 devices in a mesh: rows: 16 (over z, y), owners: 8 (over x, core).
Axes of the slice: x: 4, y: 4, z: 4, core: 2. Of those that a mesh axis runs over, the one named last changes fastest.
Arguments:
- instrument_feature_matrix: bfloat16 [131072, 1024], P(('rows', 'owners')), may hold values from -11 to 11
- partition_prototypes: float32 [1024, 1024], replicated, may hold values from -1.5 to 1.5
- softmax_sharpness_divisor: float32 [1], replicated, may hold values from 8 to 16
- chosen_partition_label: int32 [131072], P(('rows', 'owners')), may hold values from 0 to 1023, as said below
- partition_holder_team: int32 [1024], replicated, may hold values from 0 to 7, as said below
- orthogonal_quantizer_turn: bfloat16 [1024, 1024], replicated, may hold values from -0.1875 to 0.1875
Outputs:
- routed: bfloat16 [524288, 1024], P(('rows', 'owners'))
- new_centroids: float32 [1024, 1024], replicated
Inputs may be any that keep to these rules, and one draw needn't show every extreme that they name: `partition_holder_team`: every owner group owns at least one cluster; the groups own unequal numbers of clusters. `chosen_partition_label`: among the rows of one device at most 512 have clusters of one owner group, and for every index along rows one owner group receives exactly 512 rows from each of the 8 devices of that index.
All inputs are finite; a program needn't handle non-finite values.
Results may differ from a plain program's by a relative error of at most 0.0035.
The roundings to bfloat16 on the way count: a program that leaves them out, or rounds other values in their place, can miss the bound.
Values may be sent and summed in bfloat16 or wider, within the bound.
No kernel may reach another device: no remote copies, remote signals or barrier semaphores. Data moves between devices by JAX's collectives and lax.ppermute only.
A program may use at most 128 MiB of HBM per device.

v0:
```python
import jax
import jax.numpy as jnp
from jax import lax
from jax.sharding import PartitionSpec as P

CAP = 512


PRIOR = 32.0


def _ring(axis, shift):
    if axis == "y":
        return "rows", [(z * 4 + y, z * 4 + (y + shift) % 4) for z in range(4) for y in range(4)]
    if axis == "z":
        return "rows", [(z * 4 + y, ((z + shift) % 4) * 4 + y) for z in range(4) for y in range(4)]
    return "owners", [(x * 2 + c, ((x + shift) % 4) * 2 + c) for x in range(4) for c in range(2)]


def _place(axis):
    if axis == "y":
        return lax.axis_index("rows") % 4
    if axis == "z":
        return lax.axis_index("rows") // 4
    return lax.axis_index("owners") // 2


_CORES = [(s, s ^ 1) for s in range(8)]


def _scatter_sum(d, axis):
    if axis == "core":
        me = lax.axis_index("owners") % 2
        halves = d.reshape(2, d.shape[0] // 2, d.shape[1])
        mine = lax.dynamic_index_in_dim(halves, me, 0, keepdims=False)
        other = lax.dynamic_index_in_dim(halves, 1 - me, 0, keepdims=False)
        return mine + lax.ppermute(other, "owners", _CORES)
    me = _place(axis)
    pieces = d.reshape(4, d.shape[0] // 4, d.shape[1])
    acc = lax.dynamic_index_in_dim(pieces, me, 0, keepdims=False)
    for shift in (1, 2, 3):
        name, perm = _ring(axis, shift)
        piece = lax.dynamic_index_in_dim(pieces, (me + shift) % 4, 0, keepdims=False)
        acc = acc + lax.ppermute(piece, name, perm)
    return acc


def _gather(d, axis):
    if axis == "core":
        me = lax.axis_index("owners") % 2
        out = jnp.zeros((2,) + d.shape, d.dtype)
        out = lax.dynamic_update_index_in_dim(out, d, me, 0)
        out = lax.dynamic_update_index_in_dim(out, lax.ppermute(d, "owners", _CORES), 1 - me, 0)
        return out.reshape(2 * d.shape[0], d.shape[1])
    me = _place(axis)
    out = jnp.zeros((4,) + d.shape, d.dtype)
    out = lax.dynamic_update_index_in_dim(out, d, me, 0)
    for shift in (1, 2, 3):
        name, perm = _ring(axis, shift)
        out = lax.dynamic_update_index_in_dim(out, lax.ppermute(d, name, perm), (me - shift) % 4, 0)
    return out.reshape(4 * d.shape[0], d.shape[1])


def _all_sum(d):
    order = ("core", "y", "z", "x")
    for axis in order:
        d = _scatter_sum(d, axis)
    for axis in reversed(order):
        d = _gather(d, axis)
    return d


def shards(
    instrument_feature_matrix,
    partition_prototypes,
    softmax_sharpness_divisor,
    chosen_partition_label,
    partition_holder_team,
    orthogonal_quantizer_turn,
):
    groups = lax.axis_size("owners")
    clusters, width = partition_prototypes.shape
    rows = instrument_feature_matrix.shape[0]
    x = instrument_feature_matrix
    labels = chosen_partition_label

    cent_bf = partition_prototypes.astype(jnp.bfloat16)
    prototype_length_squared_term = jnp.sum(partition_prototypes * partition_prototypes, axis=1)
    pairwise_dot_matrix = jnp.dot(x, cent_bf.T, preferred_element_type=jnp.float32)
    partition_affinity_logits = (
        2.0 * pairwise_dot_matrix - prototype_length_squared_term[None, :]
    ) / softmax_sharpness_divisor[0]
    weights = jax.nn.softmax(partition_affinity_logits, axis=1)
    weights_bf = weights.astype(jnp.bfloat16)
    part_counts = jnp.sum(weights, axis=0)
    pad = (-(clusters + 1)) % 128 + 1
    weights_wide = jnp.pad(weights_bf, ((0, 0), (0, pad)))
    packed = lax.dot_general(
        weights_wide, x, (((0,), (0,)), ((), ())), preferred_element_type=jnp.float32
    )
    packed = lax.dynamic_update_slice(packed, part_counts.reshape(1, width), (clusters, 0))
    total = _all_sum(packed)
    packed, x, labels = lax.optimization_barrier((packed, x, labels))

    owner_group = jnp.take(partition_holder_team, labels, axis=0, mode="clip")
    onehot = (owner_group[:, None] == jnp.arange(groups, dtype=jnp.int32)[None, :]).astype(jnp.int32)
    before = jnp.cumsum(onehot, axis=0) - onehot
    rank_in_group = jnp.sum(before * onehot, axis=1)
    slot_index = owner_group * CAP + rank_in_group
    source_row = (
        jnp.zeros((groups * CAP,), jnp.int32).at[slot_index].set(jnp.arange(rows, dtype=jnp.int32))
    )
    slot_label = jnp.full((groups * CAP,), -1, jnp.int32).at[slot_index].set(labels)
    slot_x = jnp.take(x, source_row, axis=0, mode="clip")
    recv_x = lax.all_to_all(
        slot_x.reshape(groups, CAP, width), "owners", split_axis=0, concat_axis=0, tiled=True
    ).reshape(groups * CAP, width)
    recv_label = lax.all_to_all(
        slot_label.reshape(groups, CAP), "owners", split_axis=0, concat_axis=0, tiled=True
    ).reshape(groups * CAP)

    valid = recv_label >= 0
    chooser = (recv_label[:, None] == jnp.arange(clusters, dtype=jnp.int32)[None, :]).astype(
        jnp.bfloat16
    )
    chooser = jnp.concatenate([chooser, chooser], axis=1)

    total_sums = total[:clusters]
    total_counts = total[clusters]
    new_centroids = (total_sums + PRIOR * partition_prototypes) * (
        1.0 / (total_counts + PRIOR)
    )[:, None]
    high = lax.reduce_precision(new_centroids, exponent_bits=8, mantissa_bits=7)
    low = (new_centroids - high).astype(jnp.bfloat16)
    picked = jnp.dot(
        chooser,
        jnp.concatenate([high.astype(jnp.bfloat16), low], axis=0),
        preferred_element_type=jnp.float32,
    )
    residual_vectors = (recv_x.astype(jnp.float32) - picked).astype(jnp.bfloat16)
    residual_vectors = jnp.where(valid[:, None], residual_vectors, jnp.zeros_like(residual_vectors))
    routed = jnp.dot(
        residual_vectors, orthogonal_quantizer_turn, preferred_element_type=jnp.float32
    ).astype(jnp.bfloat16)
    return (routed, new_centroids)


def solution(mesh):
    return jax.shard_map(
        shards,
        mesh=mesh,
        in_specs=(P(("rows", "owners"), None), P(), P(), P(("rows", "owners")), P(), P()),
        out_specs=(P(("rows", "owners"), None), P()),
        check_vma=False,
    )
```

profile of v0, /device:TPU:1, one launch (start us, length us, event | category | flops | bytes accessed | tf_op | source)
XLA Modules:
  0.0 287.0 jit_solution(2603533408107422754)
XLA Ops:
  1.5 2.9 %multiply_reduce_fusion = f32[1024]{0:T(1024)S(1)} fusion(f32[1024,1024]{1,0:T(8,128)} %param.7), kind=kLoop, calls=%fused_computation.26 | loop fusion | flops 2096128 | bytes 4198400 | tf_op jit(solution)/shard_map/reduce_sum | solution.py:88
  4.7 2.4 fusion.56
  7.8 0.8 fusion.31
  8.6 4.2 %fusion.28 = f32[1152,1024]{1,0:T(8,128)} fusion(bf16[1024,1024]{1,0:T(8,128)(2,1)S(1)} %copy-done, bf16[1024,1024]{0,1:T(8,128)(2,1)S(1)} %get-tuple-element.11), kind=kOutput, calls=%fused_computation.33 | convolution fusion | flops 2415919104 | bytes 8912896 | tf_op jit(solution)/shard_map/dot_general | solution.py:98
  12.8 1.4 dynamic_update_slice.49
  14.2 3.4 %dynamic-slice_bitcast_fusion = f32[576,1024]{1,0:T(8,128)} fusion(f32[2,576,1024]{2,1,0:T(8,128)} %bitcast.115, s32[]{:T(128)S(6)} %select_n.196), kind=kLoop, calls=%fused_computation.32 | loop fusion | bytes 4718596 | tf_op jit(solution)/shard_map/jit(dynamic_index_in_dim)/squeeze | solution.py:36
  17.6 1.4 collective-permute-start
  19.0 4.5 %gather_fusion = s32[1024]{0:T(1024)S(1)} fusion(s32[1024]{0:T(1024)S(1)} %copy-done.2, s32[1024]{0:T(1024)S(1)} %broadcast_clamp_fusion.1), kind=kCustom, calls=%fused_computation | custom fusion | bytes 12288 | tf_op jit(solution)/shard_map/jit(_take)/gather | solution.py:105
  23.5 2.3 reduce-window.6
  26.3 2.8 bitcast_add_fusion
  29.1 1.4 copy-done.6
  30.5 1.2 dynamic-slice_bitcast_fusion.3
  31.7 1.4 collective-permute-start.1
  33.1 1.4 collective-permute-start.3
  34.5 1.6 collective-permute-start.2
  36.3 4.9 %scatter_custom_fusion = s32[4096]{0:T(1024)} fusion(s32[1024]{0:T(1024)S(1)} %bitcast.124, s32[1024]{0:T(1024)S(1)} %copy-done.8, s32[]{:T(128)} %constant.230.clone.1), kind=kCustom, calls=%fused_computation.80 | custom fusion | bytes 16388 | tf_op jit(solution)/shard_map/scatter | solution.py:113
  41.2 5.1 %all-to-all-start = ((s32[8,1,512]{2,1,0:T(1,128)}), s32[8,1,512]{2,1,0:T(1,128)S(1)}, u32[]{:S(2)}, u32[]{:S(2)}) async-start(s32[8,1,512]{2,1,0:T(1,128)} %bitcast.6), calls=%async_computation | async-start | bytes 32768 | tf_op jit(solution)/shard_map/all_to_all | solution.py:118
  46.3 4.3 %scatter_custom_fusion.1 = s32[4096]{0:T(1024)S(1)} fusion(s32[1024]{0:T(1024)S(1)} %bitcast.125, s32[1024]{0:T(1024)S(1)} %iota.15, s32[]{:T(128)} %constant.236.clone.1), kind=kCustom, calls=%fused_computation.77 | custom fusion | bytes 16388 | tf_op jit(solution)/shard_map/scatter | solution.py:111
  51.5 10.6 %collective-permute-done.2 = f32[144,1024]{1,0:T(8,128)} collective-permute-done((f32[144,1024]{1,0:T(8,128)S(1)}, f32[144,1024]{1,0:T(8,128)}, u32[]{:S(2)}, u32[]{:S(2)}) %collective-permute-start.2) | collective-permute-done | bytes 589856 | tf_op jit(solution)/shard_map/ppermute | solution.py:44
  62.1 1.8 fusion.34
  64.6 1.6 collective-permute-start.4
  66.3 2.1 collective-permute-start.6
  68.4 1.3 collective-permute-start.5
  69.7 18.1 %gather_fusion.1 = bf16[4096,1024]{1,0:T(8,128)(2,1)} fusion(bf16[1024,1024]{1,0:T(8,128)(2,1)S(1)} %copy-done, s32[4096]{0:T(1024)S(1)} %broadcast_clamp_fusion), kind=kCustom, calls=%fused_computation.1 | custom fusion | bytes 16793600 | tf_op jit(solution)/shard_map/jit(_take)/gather | solution.py:114
  87.8 6.7 %all-to-all-start.1 = ((bf16[8,512,1024]{2,1,0:T(8,128)(2,1)}), bf16[8,512,1024]{2,1,0:T(8,128)(2,1)}, u32[]{:S(2)}, u32[]{:S(2)}) async-start(bf16[8,512,1024]{2,1,0:T(8,128)(2,1)} %bitcast.108), calls=%async_computation.1 | async-start | bytes 16777216 | tf_op jit(solution)/shard_map/all_to_all | solution.py:115
  94.6 1.0 fusion.36
  95.6 1.4 collective-permute-start.7
  97.0 1.3 collective-permute-start.9
  98.3 1.7 collective-permute-start.8
  100.0 89.5 %collective-permute-done.7 = f32[9,1024]{1,0:T(8,128)S(1)} collective-permute-done((f32[9,1024]{1,0:T(8,128)S(1)}, f32[9,1024]{1,0:T(8,128)S(1)}, u32[]{:S(2)}, u32[]{:S(2)}) %collective-permute-start.7) | collective-permute-done | bytes 36896 | tf_op jit(solution)/shard_map/ppermute | solution.py:44
  189.5 1.5 collective-permute-done.8
  191.5 1.8 collective-permute-start.11
  194.0 1.8 collective-permute-done.10
  197.9 2.0 collective-permute-start.15
  200.2 2.3 collective-permute-done.13
  202.6 3.3 %collective-permute-done.14 = f32[36,1024]{1,0:T(8,128)S(1)} collective-permute-done((f32[36,1024]{1,0:T(8,128)S(1)}, f32[36,1024]{1,0:T(8,128)S(1)}, u32[]{:S(2)}, u32[]{:S(2)}) %collective-permute-start.14) | collective-permute-done | bytes 147488 | tf_op jit(solution)/shard_map/ppermute | solution.py:60
  206.0 0.9 collective-permute-start.16
  207.0 1.8 collective-permute-start.17
  209.9 8.7 %collective-permute-done.16 = f32[144,1024]{1,0:T(8,128)S(1)} collective-permute-done((f32[144,1024]{1,0:T(8,128)S(1)}, f32[144,1024]{1,0:T(8,128)S(1)}, u32[]{:S(2)}, u32[]{:S(2)}) %collective-permute-start.16) | collective-permute-done | bytes 589856 | tf_op jit(solution)/shard_map/ppermute | solution.py:60
  218.7 12.6 %collective-permute-done.17 = f32[144,1024]{1,0:T(8,128)S(1)} collective-permute-done((f32[144,1024]{1,0:T(8,128)S(1)}, f32[144,1024]{1,0:T(8,128)S(1)}, u32[]{:S(2)}, u32[]{:S(2)}) %collective-permute-start.17) | collective-permute-done | bytes 589856 | tf_op jit(solution)/shard_map/ppermute | solution.py:60
  231.4 3.4 %collective-permute-done.18 = f32[144,1024]{1,0:T(8,128)S(1)} collective-permute-done((f32[144,1024]{1,0:T(8,128)S(1)}, f32[144,1024]{1,0:T(8,128)S(1)}, u32[]{:S(2)}, u32[]{:S(2)}) %collective-permute-start.18) | collective-permute-done | bytes 589856 | tf_op jit(solution)/shard_map/ppermute | solution.py:60
  234.8 1.6 collective-permute-start.19
  236.5 4.0 %iota_compare_fusion = pred[4096,1024]{1,0:T(32,128)(4,1)} fusion(s32[4096]{0:T(1024)S(1)} %bitcast.118), kind=kLoop, calls=%fused_computation.10 | loop fusion | flops 4194304 | bytes 4210688 | tf_op jit(solution)/shard_map/eq | solution.py:123
  241.6 1.6 copy-done.4
  243.2 1.9 reduce-precision_convert_fusion
  245.1 2.0 copy-done.5
  247.8 24.3 %fusion.69 = bf16[4096,1024]{1,0:T(8,128)(2,1)} fusion(pred[4096]{0:T(1024)(128)(4,1)S(1)} %broadcast_compare_fusion, pred[4096,1024]{1,0:T(32,128)(4,1)} %iota_compare_fusion, bf16[4096,1024]{1,0:T(8,128)(2,1)} %bitcast.41, bf16[1024,1024]{1,0:T(8,128)(2,1)S(1)} %fusion.17, bf16[1024,1024]{1,0:T(8,128)(2,1)} %get-tuple-element.6), kind=kOutput, calls=%fused_computation.12.clone.clone.clone.1 | convolution fusion | flops 17213423616 | bytes 25169920 | tf_op jit(solution)/shard_map/dot_general | solution.py:135
  272.2 14.8 %fusion.10 = bf16[4096,1024]{1,0:T(8,128)(2,1)} fusion(bf16[1024,1024]{1,0:T(8,128)(2,1)S(1)} %copy-done.9, bf16[4096,1024]{1,0:T(8,128)(2,1)} %fusion.69), kind=kOutput, calls=%fused_computation.14 | convolution fusion | flops 8594128896 | bytes 18874368 | tf_op jit(solution)/shard_map/dot_general | solution.py:142
  (75 shorter events, 10.0 us)
Async XLA Ops:
  0.6 3.8 %copy-start = (bf16[1024,1024]{1,0:T(8,128)(2,1)S(1)}, bf16[1024,1024]{1,0:T(8,128)(2,1)}, u32[]{:S(2)}) copy-start(bf16[1024,1024]{1,0:T(8,128)(2,1)} %param.6) | copy-start | bytes 6291460
  0.7 4.1 %copy-start.3 = (f32[1024,1024]{1,0:T(8,128)S(1)}, f32[1024,1024]{1,0:T(8,128)}, u32[]{:S(2)}) copy-start(f32[1024,1024]{1,0:T(8,128)} %param.7) | copy-start | bytes 12582916
  12.8 6.2 %copy-start.8 = (s32[1024]{0:T(1024)S(1)}, s32[1024]{0:T(1024)}, u32[]{:S(2)}) copy-start(s32[1024]{0:T(1024)} %param.9) | copy-start | bytes 12292
  12.8 6.2 %copy-start.2 = (s32[1024]{0:T(1024)S(1)}, s32[1024]{0:T(1024)}, u32[]{:S(2)}) copy-start(s32[1024]{0:T(1024)} %param.10) | copy-start | bytes 12292
  17.6 8.7 %collective-permute-start = (f32[576,1024]{1,0:T(8,128)}, f32[576,1024]{1,0:T(8,128)}, u32[]{:S(2)}, u32[]{:S(2)}) collective-permute-start(f32[576,1024]{1,0:T(8,128)} %dynamic-slice_bitcast_fusion), channel_id=1, source_target_pairs={{0,1},{1,0},{2,3},{3,2},{4,5},{5,4},{6,7},{7,6},{8,9},{9,8},{10,11... | collective-permute-start | bytes 7077896 | tf_op jit(solution)/shard_map/ppermute | solution.py:37
  29.1 1.4 copy-start.6
  31.7 19.0 %collective-permute-start.1 = (f32[144,1024]{1,0:T(8,128)}, f32[144,1024]{1,0:T(8,128)S(1)}, u32[]{:S(2)}, u32[]{:S(2)}) collective-permute-start(f32[144,1024]{1,0:T(8,128)} %get-tuple-element.12), channel_id=1, source_target_pairs={{0,8},{8,16},{16,24},{24,0},{32,40},{40,48},{48,56},{56,32},{64,72... | collective-permute-start | bytes 1769480 | tf_op jit(solution)/shard_map/ppermute | solution.py:44
  33.1 17.6 %collective-permute-start.3 = (f32[144,1024]{1,0:T(8,128)}, f32[144,1024]{1,0:T(8,128)}, u32[]{:S(2)}, u32[]{:S(2)}) collective-permute-start(f32[144,1024]{1,0:T(8,128)} %get-tuple-element.13), channel_id=1, source_target_pairs={{0,24},{8,0},{16,8},{24,16},{32,56},{40,32},{48,40},{56,48},{64,88... | collective-permute-start | bytes 1769480 | tf_op jit(solution)/shard_map/ppermute | solution.py:44
  34.5 27.5 %collective-permute-start.2 = (f32[144,1024]{1,0:T(8,128)S(1)}, f32[144,1024]{1,0:T(8,128)}, u32[]{:S(2)}, u32[]{:S(2)}) collective-permute-start(f32[144,1024]{1,0:T(8,128)S(1)} %get-tuple-element.14), channel_id=1, source_target_pairs={{0,16},{8,24},{16,0},{24,8},{32,48},{40,56},{48,32},{56,40},{64,80... | collective-permute-start | bytes 1769480 | tf_op jit(solution)/shard_map/ppermute | solution.py:44
  41.2 46.7 %all-to-all-start = ((s32[8,1,512]{2,1,0:T(1,128)}), s32[8,1,512]{2,1,0:T(1,128)S(1)}, u32[]{:S(2)}, u32[]{:S(2)}) async-start(s32[8,1,512]{2,1,0:T(1,128)} %bitcast.6), calls=%async_computation | async-start | bytes 32768 | tf_op jit(solution)/shard_map/all_to_all | solution.py:118
  50.7 0.8 copy-start.7
  64.6 29.9 %collective-permute-start.4 = (f32[36,1024]{1,0:T(8,128)}, f32[36,1024]{1,0:T(8,128)S(1)}, u32[]{:S(2)}, u32[]{:S(2)}) collective-permute-start(f32[36,1024]{1,0:T(8,128)} %get-tuple-element.15), channel_id=1, source_target_pairs={{0,32},{8,40},{16,48},{24,56},{32,64},{40,72},{48,80},{56,88},{64,... | collective-permute-start | bytes 442376 | tf_op jit(solution)/shard_map/ppermute | solution.py:44
  66.3 28.3 %collective-permute-start.6 = (f32[36,1024]{1,0:T(8,128)S(1)}, f32[36,1024]{1,0:T(8,128)S(1)}, u32[]{:S(2)}, u32[]{:S(2)}) collective-permute-start(f32[36,1024]{1,0:T(8,128)S(1)} %get-tuple-element.16), channel_id=1, source_target_pairs={{0,96},{8,104},{16,112},{24,120},{32,0},{40,8},{48,16},{56,24},{64... | collective-permute-start | bytes 442376 | tf_op jit(solution)/shard_map/ppermute | solution.py:44
  68.4 26.2 %collective-permute-start.5 = (f32[36,1024]{1,0:T(8,128)S(1)}, f32[36,1024]{1,0:T(8,128)}, u32[]{:S(2)}, u32[]{:S(2)}) collective-permute-start(f32[36,1024]{1,0:T(8,128)S(1)} %get-tuple-element.17), channel_id=1, source_target_pairs={{0,64},{8,72},{16,80},{24,88},{32,96},{40,104},{48,112},{56,120},{... | collective-permute-start | bytes 442376 | tf_op jit(solution)/shard_map/ppermute | solution.py:44
  87.8 160.0 %all-to-all-start.1 = ((bf16[8,512,1024]{2,1,0:T(8,128)(2,1)}), bf16[8,512,1024]{2,1,0:T(8,128)(2,1)}, u32[]{:S(2)}, u32[]{:S(2)}) async-start(bf16[8,512,1024]{2,1,0:T(8,128)(2,1)} %bitcast.108), calls=%async_computation.1 | async-start | bytes 16777216 | tf_op jit(solution)/shard_map/all_to_all | solution.py:115
  95.6 93.9 %collective-permute-start.7 = (f32[9,1024]{1,0:T(8,128)S(1)}, f32[9,1024]{1,0:T(8,128)S(1)}, u32[]{:S(2)}, u32[]{:S(2)}) collective-permute-start(f32[9,1024]{1,0:T(8,128)S(1)} %get-tuple-element.18), channel_id=1, source_target_pairs={{0,2},{1,3},{2,4},{3,5},{4,6},{5,7},{6,0},{7,1},{8,10},{9,11},{10,... | collective-permute-start | bytes 110600 | tf_op jit(solution)/shard_map/ppermute | solution.py:44
  97.0 92.5 %collective-permute-start.9 = (f32[9,1024]{1,0:T(8,128)S(1)}, f32[9,1024]{1,0:T(8,128)S(1)}, u32[]{:S(2)}, u32[]{:S(2)}) collective-permute-start(f32[9,1024]{1,0:T(8,128)S(1)} %get-tuple-element.19), channel_id=1, source_target_pairs={{0,6},{1,7},{2,0},{3,1},{4,2},{5,3},{6,4},{7,5},{8,14},{9,15},{10,... | collective-permute-start | bytes 110600 | tf_op jit(solution)/shard_map/ppermute | solution.py:44
  98.3 92.7 %collective-permute-start.8 = (f32[9,1024]{1,0:T(8,128)S(1)}, f32[9,1024]{1,0:T(8,128)S(1)}, u32[]{:S(2)}, u32[]{:S(2)}) collective-permute-start(f32[9,1024]{1,0:T(8,128)S(1)} %get-tuple-element.20), channel_id=1, source_target_pairs={{0,4},{1,5},{2,6},{3,7},{4,0},{5,1},{6,2},{7,3},{8,12},{9,13},{10,... | collective-permute-start | bytes 110600 | tf_op jit(solution)/shard_map/ppermute | solution.py:44
  191.1 4.7 %collective-permute-start.10 = (f32[9,1024]{1,0:T(8,128)S(1)}, f32[9,1024]{1,0:T(8,128)S(1)}, u32[]{:S(2)}, u32[]{:S(2)}) collective-permute-start(f32[9,1024]{1,0:T(8,128)S(1)} %get-tuple-element.9), channel_id=1, source_target_pairs={{0,2},{1,3},{2,4},{3,5},{4,6},{5,7},{6,0},{7,1},{8,10},{9,11},{10,... | collective-permute-start | bytes 110600 | tf_op jit(solution)/shard_map/ppermute | solution.py:60
  191.5 5.1 %collective-permute-start.11 = (f32[9,1024]{1,0:T(8,128)S(1)}, f32[9,1024]{1,0:T(8,128)S(1)}, u32[]{:S(2)}, u32[]{:S(2)}) collective-permute-start(f32[9,1024]{1,0:T(8,128)S(1)} %get-tuple-element.9), channel_id=1, source_target_pairs={{0,4},{1,5},{2,6},{3,7},{4,0},{5,1},{6,2},{7,3},{8,12},{9,13},{10,... | collective-permute-start | bytes 110600 | tf_op jit(solution)/shard_map/ppermute | solution.py:60
  193.2 3.8 %collective-permute-start.12 = (f32[9,1024]{1,0:T(8,128)S(1)}, f32[9,1024]{1,0:T(8,128)S(1)}, u32[]{:S(2)}, u32[]{:S(2)}) collective-permute-start(f32[9,1024]{1,0:T(8,128)S(1)} %get-tuple-element.9), channel_id=1, source_target_pairs={{0,6},{1,7},{2,0},{3,1},{4,2},{5,3},{6,4},{7,5},{8,14},{9,15},{10,... | collective-permute-start | bytes 110600 | tf_op jit(solution)/shard_map/ppermute | solution.py:60
  197.1 5.4 %collective-permute-start.13 = (f32[36,1024]{1,0:T(8,128)S(1)}, f32[36,1024]{1,0:T(8,128)S(1)}, u32[]{:S(2)}, u32[]{:S(2)}) collective-permute-start(f32[36,1024]{1,0:T(8,128)S(1)} %reshape.118), channel_id=1, source_target_pairs={{0,32},{8,40},{16,48},{24,56},{32,64},{40,72},{48,80},{56,88},{64,... | collective-permute-start | bytes 442376 | tf_op jit(solution)/shard_map/ppermute | solution.py:60
  197.9 8.0 %collective-permute-start.15 = (f32[36,1024]{1,0:T(8,128)S(1)}, f32[36,1024]{1,0:T(8,128)S(1)}, u32[]{:S(2)}, u32[]{:S(2)}) collective-permute-start(f32[36,1024]{1,0:T(8,128)S(1)} %reshape.118), channel_id=1, source_target_pairs={{0,96},{8,104},{16,112},{24,120},{32,0},{40,8},{48,16},{56,24},{64... | collective-permute-start | bytes 442376 | tf_op jit(solution)/shard_map/ppermute | solution.py:60
  200.0 6.0 %collective-permute-start.14 = (f32[36,1024]{1,0:T(8,128)S(1)}, f32[36,1024]{1,0:T(8,128)S(1)}, u32[]{:S(2)}, u32[]{:S(2)}) collective-permute-start(f32[36,1024]{1,0:T(8,128)S(1)} %reshape.118), channel_id=1, source_target_pairs={{0,64},{8,72},{16,80},{24,88},{32,96},{40,104},{48,112},{56,120},{... | collective-permute-start | bytes 442376 | tf_op jit(solution)/shard_map/ppermute | solution.py:60
  206.0 12.6 %collective-permute-start.16 = (f32[144,1024]{1,0:T(8,128)S(1)}, f32[144,1024]{1,0:T(8,128)S(1)}, u32[]{:S(2)}, u32[]{:S(2)}) collective-permute-start(f32[144,1024]{1,0:T(8,128)S(1)} %reshape.119), channel_id=1, source_target_pairs={{0,8},{8,16},{16,24},{24,0},{32,40},{40,48},{48,56},{56,32},{64,72... | collective-permute-start | bytes 1769480 | tf_op jit(solution)/shard_map/ppermute | solution.py:60
  207.0 24.4 %collective-permute-start.17 = (f32[144,1024]{1,0:T(8,128)S(1)}, f32[144,1024]{1,0:T(8,128)S(1)}, u32[]{:S(2)}, u32[]{:S(2)}) collective-permute-start(f32[144,1024]{1,0:T(8,128)S(1)} %reshape.119), channel_id=1, source_target_pairs={{0,16},{8,24},{16,0},{24,8},{32,48},{40,56},{48,32},{56,40},{64,80... | collective-permute-start | bytes 1769480 | tf_op jit(solution)/shard_map/ppermute | solution.py:60
  208.9 25.9 %collective-permute-start.18 = (f32[144,1024]{1,0:T(8,128)S(1)}, f32[144,1024]{1,0:T(8,128)S(1)}, u32[]{:S(2)}, u32[]{:S(2)}) collective-permute-start(f32[144,1024]{1,0:T(8,128)S(1)} %reshape.119), channel_id=1, source_target_pairs={{0,24},{8,0},{16,8},{24,16},{32,56},{40,32},{48,40},{56,48},{64,88... | collective-permute-start | bytes 1769480 | tf_op jit(solution)/shard_map/ppermute | solution.py:60
  234.8 6.5 %collective-permute-start.19 = (f32[576,1024]{1,0:T(8,128)S(1)}, f32[576,1024]{1,0:T(8,128)S(1)}, u32[]{:S(2)}, u32[]{:S(2)}) collective-permute-start(f32[576,1024]{1,0:T(8,128)S(1)} %bitcast.113), channel_id=1, source_target_pairs={{0,1},{1,0},{2,3},{3,2},{4,5},{5,4},{6,7},{7,6},{8,9},{9,8},{10,11... | collective-permute-start | bytes 7077896 | tf_op jit(solution)/shard_map/ppermute | solution.py:53
  241.0 2.2 copy-start.4
  245.1 2.0 copy-start.5
  247.8 24.4 %copy-start.9 = (bf16[1024,1024]{1,0:T(8,128)(2,1)S(1)}, bf16[1024,1024]{1,0:T(8,128)(2,1)}, u32[]{:S(2)}) copy-start(bf16[1024,1024]{1,0:T(8,128)(2,1)} %param.11) | copy-start | bytes 6291460
  272.2 14.9 %copy-start.1 = (bf16[1024,1024]{1,0:T(8,128)(2,1)S(1)}, bf16[1024,1024]{1,0:T(8,128)(2,1)}, u32[]{:S(2)}) copy-start(bf16[1024,1024]{1,0:T(8,128)(2,1)} %param.6) | copy-start | bytes 6291460
where the time goes:
time: 287 us
  waiting for transfers between devices  135 us (47%)
  local copies, waits for them, and re-layouts  47 us (16%)
  matrix products  45.8 us (16%)
  starting transfers between devices  38.2 us (13%)
  other arithmetic  19.1 us (7%)
    ppermute x9, waiting for transfers between devices, _scatter_sum(): acc = acc + lax.ppermute(piece, name, perm)  102 us
    ppermute x9, waiting for transfers between devices, _gather(): lax.ppermute(d, name, perm)  33.4 us
    dot_general x1, matrix products, shards(): jnp.dot(chooser, jnp.concatenate([high.astype(jnp.bfloat16), low], axis=0...  24.3 us
    gather x1, local copies, waits for them, and re-layouts, shards(): slot_x = jnp.take(x, source_row, axis=0, mode='clip')  18.1 us
    dot_general x1, matrix products, shards(): jnp.dot(residual_vectors, orthogonal_quantizer_turn, preferred_element_ty...  14.8 us
    ppermute x9, starting transfers between devices, _scatter_sum(): acc = acc + lax.ppermute(piece, name, perm)  14 us
    ppermute x9, starting transfers between devices, _gather(): lax.ppermute(d, name, perm)  9.39 us
    all_to_all x1, starting transfers between devices, shards(): lax.all_to_all(slot_x.reshape(groups, CAP, width), 'owners', split_axis=0...  6.71 us
  transfers between devices with their start and end apart: 22, of which 11 were waited for; matrix products, arithmetic and copies ran while one was open for 16% of the time, Pallas kernels for 0%

commit v1 on v0

--- a/solution.py
+++ b/solution.py
@@ -99,8 +99,9 @@
         weights_wide, x, (((0,), (0,)), ((), ())), preferred_element_type=jnp.float32
     )
     packed = lax.dynamic_update_slice(packed, part_counts.reshape(1, width), (clusters, 0))
-    total = _all_sum(packed)
-    packed, x, labels = lax.optimization_barrier((packed, x, labels))
+    partial = packed
+    for axis in ("core", "y", "z"):
+        partial = _scatter_sum(partial, axis)
 
     owner_group = jnp.take(partition_holder_team, labels, axis=0, mode="clip")
     onehot = (owner_group[:, None] == jnp.arange(groups, dtype=jnp.int32)[None, :]).astype(jnp.int32)
@@ -112,9 +113,18 @@
     )
     slot_label = jnp.full((groups * CAP,), -1, jnp.int32).at[slot_index].set(labels)
     slot_x = jnp.take(x, source_row, axis=0, mode="clip")
-    recv_x = lax.all_to_all(
-        slot_x.reshape(groups, CAP, width), "owners", split_axis=0, concat_axis=0, tiled=True
-    ).reshape(groups * CAP, width)
+    slot_x = slot_x.reshape(groups, CAP, width)
+    half = CAP // 2
+    recv_first = lax.all_to_all(slot_x[:, :half], "owners", split_axis=0, concat_axis=0, tiled=True)
+    partial, recv_first = lax.optimization_barrier((partial, recv_first))
+    partial = _scatter_sum(partial, "x")
+    partial = _gather(partial, "x")
+    partial, second = lax.optimization_barrier((partial, slot_x[:, half:]))
+    recv_second = lax.all_to_all(second, "owners", split_axis=0, concat_axis=0, tiled=True)
+    for axis in ("z", "y", "core"):
+        partial = _gather(partial, axis)
+    total = partial
+    recv_x = jnp.concatenate([recv_first, recv_second], axis=1).reshape(groups * CAP, width)
     recv_label = lax.all_to_all(
         slot_label.reshape(groups, CAP), "owners", split_axis=0, concat_axis=0, tiled=True
     ).reshape(groups * CAP)

time: 287 us -> 279 us (0.972)
  waiting for transfers between devices: 135 us -> 100 us
  local copies, waits for them, and re-layouts: 47 us -> 56.7 us
  blocking collectives: 0 us -> 8.22 us
  other arithmetic: 19.1 us -> 25.7 us
    ppermute x9, waiting for transfers between devices: 102 us -> 36.8 us  [_scatter_sum(): acc = acc + lax.ppermute(piece, name, perm)]
    all_to_all x2, waiting for transfers between devices: 0.01 us -> 35.8 us  [the longest x1 35.3 us: shards(): lax.all_to_all(second, 'owners', split_axis=0, concat_axis=0, tiled=True)]
    all_to_all x0 -> x1, blocking collectives: none -> 8.22 us  [shards(): lax.all_to_all(slot_label.reshape(groups, CAP), 'owners', split_axis=0, c...]
    concatenate x0 -> x1, other arithmetic: none -> 7.84 us  [shards(): jnp.concatenate([recv_first, recv_second], axis=1)]
    slice x1 -> x2, local copies, waits for them, and re-layouts: 0.28 us -> 6.3 us  [the longest x1 6.02 us: shards(): partial, second = lax.optimization_barrier((partial, slot_x[:, half:]))]
    ppermute x9, waiting for transfers between devices: 33.4 us -> 27.7 us  [_gather(): lax.ppermute(d, name, perm)]
    ppermute x9, starting transfers between devices: 9.39 us -> 12.3 us  [_gather(): lax.ppermute(d, name, perm)]
    unnamed x20 -> x18, local copies, waits for them, and re-layouts: 6.15 us -> 3.77 us
  transfers between devices with their start and end apart: 22 -> 22, of which waited for: 11 -> 14; matrix products, arithmetic and copies ran while one was open for 16% -> 22% of each run, Pallas kernels for 0% -> 0%
where the time goes in v1:
time: 279 us
  waiting for transfers between devices  100 us (36%)
  local copies, waits for them, and re-layouts  56.7 us (20%)
  matrix products  46 us (16%)
  starting transfers between devices  40 us (14%)
  other arithmetic  25.7 us (9%)
  blocking collectives  8.22 us (3%)
    ppermute x9, waiting for transfers between devices, _scatter_sum(): acc = acc + lax.ppermute(piece, name, perm)  36.8 us
    all_to_all x1, waiting for transfers between devices, shards(): lax.all_to_all(second, 'owners', split_axis=0, concat_axis=0, tiled=True)  35.3 us
    ppermute x9, waiting for transfers between devices, _gather(): lax.ppermute(d, name, perm)  27.7 us
    dot_general x1, matrix products, shards(): jnp.dot(chooser, jnp.concatenate([high.astype(jnp.bfloat16), low], axis=0...  24.4 us
    gather x1, local copies, waits for them, and re-layouts, shards(): slot_x = jnp.take(x, source_row, axis=0, mode='clip')  18.1 us
    dot_general x1, matrix products, shards(): jnp.dot(residual_vectors, orthogonal_quantizer_turn, preferred_element_ty...  14.9 us
    ppermute x9, starting transfers between devices, _scatter_sum(): acc = acc + lax.ppermute(piece, name, perm)  12.8 us
    ppermute x9, starting transfers between devices, _gather(): lax.ppermute(d, name, perm)  12.3 us
  transfers between devices with their start and end apart: 22, of which 14 were waited for; matrix products, arithmetic and copies ran while one was open for 22% of the time, Pallas kernels for 0%

profile of v1, /device:TPU:1, one launch (start us, length us, event | category | flops | bytes accessed | tf_op | source)
XLA Modules:
  0.0 278.9 jit_solution(3960732250517539125)
XLA Ops:
  1.5 2.9 %multiply_reduce_fusion = f32[1024]{0:T(1024)S(1)} fusion(f32[1024,1024]{1,0:T(8,128)} %param.7), kind=kLoop, calls=%fused_computation.27 | loop fusion | flops 2096128 | bytes 4198400 | tf_op jit(solution)/shard_map/reduce_sum | solution.py:88
  4.7 2.4 fusion.57
  8.6 4.3 %fusion.28 = f32[1152,1024]{1,0:T(8,128)} fusion(bf16[1024,1024]{1,0:T(8,128)(2,1)S(1)} %copy-done, bf16[1024,1024]{0,1:T(8,128)(2,1)S(1)} %get-tuple-element.17), kind=kOutput, calls=%fused_computation.34 | convolution fusion | flops 2415919104 | bytes 8912896 | tf_op jit(solution)/shard_map/dot_general | solution.py:98
  12.9 1.4 dynamic_update_slice.49
  14.3 3.3 %dynamic-slice_bitcast_fusion = f32[576,1024]{1,0:T(8,128)} fusion(f32[2,576,1024]{2,1,0:T(8,128)} %bitcast.116, s32[]{:T(128)S(6)} %select_n.196), kind=kLoop, calls=%fused_computation.33 | loop fusion | bytes 4718596 | tf_op jit(solution)/shard_map/jit(dynamic_index_in_dim)/squeeze | solution.py:36
  17.6 1.4 collective-permute-start
  19.0 4.5 %gather_fusion = s32[1024]{0:T(1024)S(1)} fusion(s32[1024]{0:T(1024)S(1)} %copy-done.2, s32[1024]{0:T(1024)S(1)} %broadcast_clamp_fusion.1), kind=kCustom, calls=%fused_computation | custom fusion | bytes 12288 | tf_op jit(solution)/shard_map/jit(_take)/gather | solution.py:106
  23.6 2.3 reduce-window.6
  26.4 4.3 %scatter_custom_fusion.1 = s32[4096]{0:T(1024)S(1)} fusion(s32[1024]{0:T(1024)S(1)} %bitcast.126, s32[1024]{0:T(1024)S(1)} %iota.15, s32[]{:T(128)} %constant.232.clone.1), kind=kCustom, calls=%fused_computation.79 | custom fusion | bytes 16388 | tf_op jit(solution)/shard_map/scatter | solution.py:112
  30.8 18.1 %gather_fusion.1 = bf16[4096,1024]{1,0:T(8,128)(2,1)} fusion(bf16[1024,1024]{1,0:T(8,128)(2,1)S(1)} %copy-done, s32[4096]{0:T(1024)S(1)} %broadcast_clamp_fusion), kind=kCustom, calls=%fused_computation.1 | custom fusion | bytes 16793600 | tf_op jit(solution)/shard_map/jit(_take)/gather | solution.py:115
  48.9 6.0 %fusion.56 = (bf16[8,256,1024]{2,1,0:T(8,128)(2,1)}, bf16[8,256,1024]{2,1,0:T(8,128)(2,1)}) fusion(bf16[8,512,1024]{2,1,0:T(8,128)(2,1)} %bitcast.110), kind=kLoop, calls=%fused_computation.93 | loop fusion | bytes 16777216 | tf_op jit(solution)/shard_map/slice | solution.py:122
  55.0 4.5 %all-to-all-start.1 = ((bf16[8,256,1024]{2,1,0:T(8,128)(2,1)}), bf16[8,256,1024]{2,1,0:T(8,128)(2,1)}, u32[]{:S(2)}, u32[]{:S(2)}) async-start(bf16[8,256,1024]{2,1,0:T(8,128)(2,1)} %get-tuple-element.15), calls=%async_computation.1 | async-start | bytes 8388608 | tf_op jit(solution)/shard_map/all_to_all | solution.py:118
  59.6 2.8 %bitcast_add_fusion = f32[576,1024]{1,0:T(8,128)S(1)} fusion(f32[576,1024]{1,0:T(8,128)} %collective-permute-done, f32[2,576,1024]{2,1,0:T(8,128)} %bitcast.117, s32[]{:T(128)S(6)} %select_n.195), kind=kLoop, calls=%fused_computation.32 | loop fusion | flops 589824 | bytes 7077892 | tf_op jit(solution)/shard_map/add | solution.py:37
  62.4 1.4 copy-done.6
  63.9 1.5 collective-permute-start.1
  65.4 1.5 collective-permute-start.3
  66.9 1.6 collective-permute-start.2
  68.5 12.0 %collective-permute-done.1 = f32[144,1024]{1,0:T(8,128)S(1)} collective-permute-done((f32[144,1024]{1,0:T(8,128)S(1)}, f32[144,1024]{1,0:T(8,128)S(1)}, u32[]{:S(2)}, u32[]{:S(2)}) %collective-permute-start.1) | collective-permute-done | bytes 589856 | tf_op jit(solution)/shard_map/ppermute | solution.py:44
  80.5 13.6 %collective-permute-done.2 = f32[144,1024]{1,0:T(8,128)} collective-permute-done((f32[144,1024]{1,0:T(8,128)S(1)}, f32[144,1024]{1,0:T(8,128)}, u32[]{:S(2)}, u32[]{:S(2)}) %collective-permute-start.2) | collective-permute-done | bytes 589856 | tf_op jit(solution)/shard_map/ppermute | solution.py:44
  94.1 1.4 fusion.34
  95.7 1.7 collective-permute-start.4
  97.4 2.2 collective-permute-start.6
  100.8 2.5 collective-permute-done.4
  103.3 4.4 %collective-permute-done.5 = f32[36,1024]{1,0:T(8,128)S(1)} collective-permute-done((f32[36,1024]{1,0:T(8,128)S(1)}, f32[36,1024]{1,0:T(8,128)S(1)}, u32[]{:S(2)}, u32[]{:S(2)}) %collective-permute-start.5) | collective-permute-done | bytes 147488 | tf_op jit(solution)/shard_map/ppermute | solution.py:44
  108.7 2.4 collective-permute-start.9
  112.7 3.0 %collective-permute-done.8 = f32[9,1024]{1,0:T(8,128)S(1)} collective-permute-done((f32[9,1024]{1,0:T(8,128)S(1)}, f32[9,1024]{1,0:T(8,128)S(1)}, u32[]{:S(2)}, u32[]{:S(2)}) %collective-permute-start.8) | collective-permute-done | bytes 36896 | tf_op jit(solution)/shard_map/ppermute | solution.py:44
  116.0 1.4 collective-permute-start.11
  118.5 2.3 collective-permute-done.10
  121.5 3.8 %collective-permute-start.15 = (f32[36,1024]{1,0:T(8,128)S(1)}, f32[36,1024]{1,0:T(8,128)S(1)}, u32[]{:S(2)}, u32[]{:S(2)}) collective-permute-start(f32[36,1024]{1,0:T(8,128)S(1)} %reshape.117), channel_id=1, source_target_pairs={{0,96},{8,104},{16,112},{24,120},{32,0},{40,8},{48,16},{56,24},{64... | collective-permute-start | bytes 442376 | tf_op jit(solution)/shard_map/ppermute | solution.py:60
  126.1 6.3 %collective-permute-done.13 = f32[36,1024]{1,0:T(8,128)S(1)} collective-permute-done((f32[36,1024]{1,0:T(8,128)S(1)}, f32[36,1024]{1,0:T(8,128)S(1)}, u32[]{:S(2)}, u32[]{:S(2)}) %collective-permute-start.13) | collective-permute-done | bytes 147488 | tf_op jit(solution)/shard_map/ppermute | solution.py:60
  134.0 2.6 collective-permute-start.17
  137.8 1.7 broadcast_in_dim.100
  140.4 3.0 %collective-permute-done.16 = f32[144,1024]{1,0:T(8,128)S(1)} collective-permute-done((f32[144,1024]{1,0:T(8,128)S(1)}, f32[144,1024]{1,0:T(8,128)S(1)}, u32[]{:S(2)}, u32[]{:S(2)}) %collective-permute-start.16) | collective-permute-done | bytes 589856 | tf_op jit(solution)/shard_map/ppermute | solution.py:60
  144.2 12.9 %collective-permute-done.17 = f32[144,1024]{1,0:T(8,128)S(1)} collective-permute-done((f32[144,1024]{1,0:T(8,128)S(1)}, f32[144,1024]{1,0:T(8,128)S(1)}, u32[]{:S(2)}, u32[]{:S(2)}) %collective-permute-start.17) | collective-permute-done | bytes 589856 | tf_op jit(solution)/shard_map/ppermute | solution.py:60
  158.0 2.6 collective-permute-done.18
  161.5 3.8 %collective-permute-start.19 = (f32[576,1024]{1,0:T(8,128)}, f32[576,1024]{1,0:T(8,128)}, u32[]{:S(2)}, u32[]{:S(2)}) collective-permute-start(f32[576,1024]{1,0:T(8,128)} %bitcast.38), channel_id=1, source_target_pairs={{0,1},{1,0},{2,3},{3,2},{4,5},{5,4},{6,7},{7,6},{8,9},{9,8},{10,11... | collective-permute-start | bytes 7077896 | tf_op jit(solution)/shard_map/ppermute | solution.py:53
  165.3 4.3 %scatter_custom_fusion = s32[4096]{0:T(1024)S(1)} fusion(s32[1024]{0:T(1024)S(1)} %bitcast.127, s32[1024]{0:T(1024)S(1)} %copy-done.7, s32[]{:T(128)} %constant.230.clone.1), kind=kCustom, calls=%fused_computation.82 | custom fusion | bytes 16388 | tf_op jit(solution)/shard_map/scatter | solution.py:114
  169.6 8.2 %all_to_all.19 = s32[8,1,512]{2,1,0:T(1,128)S(1)} all-to-all(s32[8,1,512]{2,1,0:T(1,128)S(1)} %bitcast.120), channel_id=1, replica_groups=mesh['rows'=16,'owners'=8] {'owners'}, dimensions={0} | all-to-all | bytes 32768 | tf_op jit(solution)/shard_map/all_to_all | solution.py:128
  177.8 5.2 %all-to-all-start.2 = ((bf16[8,256,1024]{2,1,0:T(8,128)(2,1)}), bf16[8,256,1024]{2,1,0:T(8,128)(2,1)}, u32[]{:S(2)}, u32[]{:S(2)}) async-start(bf16[8,256,1024]{2,1,0:T(8,128)(2,1)} %get-tuple-element.8), calls=%async_computation.2 | async-start | bytes 8388608 | tf_op jit(solution)/shard_map/all_to_all | solution.py:123
  183.0 4.1 %iota_compare_fusion = pred[4096,1024]{1,0:T(32,128)(4,1)} fusion(s32[4096]{0:T(1024)S(1)} %bitcast.119), kind=kLoop, calls=%fused_computation.10 | loop fusion | flops 4194304 | bytes 4210688 | tf_op jit(solution)/shard_map/eq | solution.py:133
  187.6 2.2 bitcast_dynamic-update-slice_fusion.1
  189.8 2.0 bitcast_dynamic-update-slice_fusion
  191.9 1.9 reduce-precision_convert_fusion
  193.8 2.0 copy-done.5
  196.5 35.3 %all-to-all-done.2 = bf16[8,256,1024]{2,1,0:T(8,128)(2,1)} async-done(((bf16[8,256,1024]{2,1,0:T(8,128)(2,1)}), bf16[8,256,1024]{2,1,0:T(8,128)(2,1)}, u32[]{:S(2)}, u32[]{:S(2)}) %all-to-all-start.2) | async-done | bytes 4194336 | tf_op jit(solution)/shard_map/all_to_all | solution.py:123
  231.8 7.8 %pad_maximum_fusion = bf16[8,512,1024]{2,1,0:T(8,128)(2,1)} fusion(bf16[8,256,1024]{2,1,0:T(8,128)(2,1)} %all-to-all-done.2, bf16[8,256,1024]{2,1,0:T(8,128)(2,1)} %all-to-all-done.1), kind=kLoop, calls=%fused_computation.11 | loop fusion | flops 16777216 | bytes 16777216 | tf_op jit(solution)/shard_map/concatenate | solution.py:127
  239.6 24.4 %fusion.70 = bf16[4096,1024]{1,0:T(8,128)(2,1)} fusion(pred[4096]{0:T(1024)(128)(4,1)S(1)} %broadcast_compare_fusion, pred[4096,1024]{1,0:T(32,128)(4,1)} %iota_compare_fusion, bf16[4096,1024]{1,0:T(8,128)(2,1)} %bitcast.115, bf16[1024,1024]{1,0:T(8,128)(2,1)S(1)} %fusion.17, bf16[1024,1024]{1,0:T(8,128)(2,1)} %get-tuple-element.10), kind=kOutput, calls=%fused_computation.13.clone.clone.clone.1 | convolution fusion | flops 17213423616 | bytes 25169920 | tf_op jit(solution)/shard_map/dot_general | solution.py:145
  264.0 14.9 %fusion.10 = bf16[4096,1024]{1,0:T(8,128)(2,1)} fusion(bf16[1024,1024]{1,0:T(8,128)(2,1)S(1)} %copy-done.8, bf16[4096,1024]{1,0:T(8,128)(2,1)} %fusion.70), kind=kOutput, calls=%fused_computation.15 | convolution fusion | flops 8594128896 | bytes 18874368 | tf_op jit(solution)/shard_map/dot_general | solution.py:152
  (75 shorter events, 16.5 us)
Async XLA Ops:
  0.6 3.8 %copy-start = (bf16[1024,1024]{1,0:T(8,128)(2,1)S(1)}, bf16[1024,1024]{1,0:T(8,128)(2,1)}, u32[]{:S(2)}) copy-start(bf16[1024,1024]{1,0:T(8,128)(2,1)} %param.6) | copy-start | bytes 6291460
  0.7 4.1 %copy-start.3 = (f32[1024,1024]{1,0:T(8,128)S(1)}, f32[1024,1024]{1,0:T(8,128)}, u32[]{:S(2)}) copy-start(f32[1024,1024]{1,0:T(8,128)} %param.7) | copy-start | bytes 12582916
  12.9 6.1 %copy-start.7 = (s32[1024]{0:T(1024)S(1)}, s32[1024]{0:T(1024)}, u32[]{:S(2)}) copy-start(s32[1024]{0:T(1024)} %param.9) | copy-start | bytes 12292
  12.9 6.1 %copy-start.2 = (s32[1024]{0:T(1024)S(1)}, s32[1024]{0:T(1024)}, u32[]{:S(2)}) copy-start(s32[1024]{0:T(1024)} %param.10) | copy-start | bytes 12292
  17.6 41.9 %collective-permute-start = (f32[576,1024]{1,0:T(8,128)}, f32[576,1024]{1,0:T(8,128)}, u32[]{:S(2)}, u32[]{:S(2)}) collective-permute-start(f32[576,1024]{1,0:T(8,128)} %dynamic-slice_bitcast_fusion), channel_id=1, source_target_pairs={{0,1},{1,0},{2,3},{3,2},{4,5},{5,4},{6,7},{7,6},{8,9},{9,8},{10,11... | collective-permute-start | bytes 7077896 | tf_op jit(solution)/shard_map/ppermute | solution.py:37
  55.0 53.3 %all-to-all-start.1 = ((bf16[8,256,1024]{2,1,0:T(8,128)(2,1)}), bf16[8,256,1024]{2,1,0:T(8,128)(2,1)}, u32[]{:S(2)}, u32[]{:S(2)}) async-start(bf16[8,256,1024]{2,1,0:T(8,128)(2,1)} %get-tuple-element.15), calls=%async_computation.1 | async-start | bytes 8388608 | tf_op jit(solution)/shard_map/all_to_all | solution.py:118
  62.4 1.4 copy-start.6
  63.9 16.6 %collective-permute-start.1 = (f32[144,1024]{1,0:T(8,128)S(1)}, f32[144,1024]{1,0:T(8,128)S(1)}, u32[]{:S(2)}, u32[]{:S(2)}) collective-permute-start(f32[144,1024]{1,0:T(8,128)S(1)} %get-tuple-element.18), channel_id=1, source_target_pairs={{0,8},{8,16},{16,24},{24,0},{32,40},{40,48},{48,56},{56,32},{64,72... | collective-permute-start | bytes 1769480 | tf_op jit(solution)/shard_map/ppermute | solution.py:44
  65.4 15.1 %collective-permute-start.3 = (f32[144,1024]{1,0:T(8,128)S(1)}, f32[144,1024]{1,0:T(8,128)S(1)}, u32[]{:S(2)}, u32[]{:S(2)}) collective-permute-start(f32[144,1024]{1,0:T(8,128)S(1)} %get-tuple-element.19), channel_id=1, source_target_pairs={{0,24},{8,0},{16,8},{24,16},{32,56},{40,32},{48,40},{56,48},{64,88... | collective-permute-start | bytes 1769480 | tf_op jit(solution)/shard_map/ppermute | solution.py:44
  66.9 27.2 %collective-permute-start.2 = (f32[144,1024]{1,0:T(8,128)S(1)}, f32[144,1024]{1,0:T(8,128)}, u32[]{:S(2)}, u32[]{:S(2)}) collective-permute-start(f32[144,1024]{1,0:T(8,128)S(1)} %get-tuple-element.20), channel_id=1, source_target_pairs={{0,16},{8,24},{16,0},{24,8},{32,48},{40,56},{48,32},{56,40},{64,80... | collective-permute-start | bytes 1769480 | tf_op jit(solution)/shard_map/ppermute | solution.py:44
  95.7 7.6 %collective-permute-start.4 = (f32[36,1024]{1,0:T(8,128)S(1)}, f32[36,1024]{1,0:T(8,128)S(1)}, u32[]{:S(2)}, u32[]{:S(2)}) collective-permute-start(f32[36,1024]{1,0:T(8,128)S(1)} %get-tuple-element.21), channel_id=1, source_target_pairs={{0,32},{8,40},{16,48},{24,56},{32,64},{40,72},{48,80},{56,88},{64,... | collective-permute-start | bytes 442376 | tf_op jit(solution)/shard_map/ppermute | solution.py:44
  97.4 5.9 %collective-permute-start.6 = (f32[36,1024]{1,0:T(8,128)S(1)}, f32[36,1024]{1,0:T(8,128)S(1)}, u32[]{:S(2)}, u32[]{:S(2)}) collective-permute-start(f32[36,1024]{1,0:T(8,128)S(1)} %get-tuple-element.22), channel_id=1, source_target_pairs={{0,96},{8,104},{16,112},{24,120},{32,0},{40,8},{48,16},{56,24},{64... | collective-permute-start | bytes 442376 | tf_op jit(solution)/shard_map/ppermute | solution.py:44
  99.6 8.1 %collective-permute-start.5 = (f32[36,1024]{1,0:T(8,128)S(1)}, f32[36,1024]{1,0:T(8,128)S(1)}, u32[]{:S(2)}, u32[]{:S(2)}) collective-permute-start(f32[36,1024]{1,0:T(8,128)S(1)} %get-tuple-element.23), channel_id=1, source_target_pairs={{0,64},{8,72},{16,80},{24,88},{32,96},{40,104},{48,112},{56,120},{... | collective-permute-start | bytes 442376 | tf_op jit(solution)/shard_map/ppermute | solution.py:44
  108.3 4.4 %collective-permute-start.7 = (f32[9,1024]{1,0:T(8,128)S(1)}, f32[9,1024]{1,0:T(8,128)S(1)}, u32[]{:S(2)}, u32[]{:S(2)}) collective-permute-start(f32[9,1024]{1,0:T(8,128)S(1)} %get-tuple-element.24), channel_id=1, source_target_pairs={{0,2},{1,3},{2,4},{3,5},{4,6},{5,7},{6,0},{7,1},{8,10},{9,11},{10,... | collective-permute-start | bytes 110600 | tf_op jit(solution)/shard_map/ppermute | solution.py:44
  108.7 4.0 %collective-permute-start.9 = (f32[9,1024]{1,0:T(8,128)S(1)}, f32[9,1024]{1,0:T(8,128)S(1)}, u32[]{:S(2)}, u32[]{:S(2)}) collective-permute-start(f32[9,1024]{1,0:T(8,128)S(1)} %get-tuple-element.25), channel_id=1, source_target_pairs={{0,6},{1,7},{2,0},{3,1},{4,2},{5,3},{6,4},{7,5},{8,14},{9,15},{10,... | collective-permute-start | bytes 110600 | tf_op jit(solution)/shard_map/ppermute | solution.py:44
  111.1 4.7 %collective-permute-start.8 = (f32[9,1024]{1,0:T(8,128)S(1)}, f32[9,1024]{1,0:T(8,128)S(1)}, u32[]{:S(2)}, u32[]{:S(2)}) collective-permute-start(f32[9,1024]{1,0:T(8,128)S(1)} %get-tuple-element.26), channel_id=1, source_target_pairs={{0,4},{1,5},{2,6},{3,7},{4,0},{5,1},{6,2},{7,3},{8,12},{9,13},{10,... | collective-permute-start | bytes 110600 | tf_op jit(solution)/shard_map/ppermute | solution.py:44
  115.8 5.1 %collective-permute-start.10 = (f32[9,1024]{1,0:T(8,128)S(1)}, f32[9,1024]{1,0:T(8,128)S(1)}, u32[]{:S(2)}, u32[]{:S(2)}) collective-permute-start(f32[9,1024]{1,0:T(8,128)S(1)} %get-tuple-element.13), channel_id=1, source_target_pairs={{0,2},{1,3},{2,4},{3,5},{4,6},{5,7},{6,0},{7,1},{8,10},{9,11},{10,... | collective-permute-start | bytes 110600 | tf_op jit(solution)/shard_map/ppermute | solution.py:60
  116.0 4.9 %collective-permute-start.11 = (f32[9,1024]{1,0:T(8,128)S(1)}, f32[9,1024]{1,0:T(8,128)S(1)}, u32[]{:S(2)}, u32[]{:S(2)}) collective-permute-start(f32[9,1024]{1,0:T(8,128)S(1)} %get-tuple-element.13), channel_id=1, source_target_pairs={{0,4},{1,5},{2,6},{3,7},{4,0},{5,1},{6,2},{7,3},{8,12},{9,13},{10,... | collective-permute-start | bytes 110600 | tf_op jit(solution)/shard_map/ppermute | solution.py:60
  117.4 4.1 %collective-permute-start.12 = (f32[9,1024]{1,0:T(8,128)S(1)}, f32[9,1024]{1,0:T(8,128)S(1)}, u32[]{:S(2)}, u32[]{:S(2)}) collective-permute-start(f32[9,1024]{1,0:T(8,128)S(1)} %get-tuple-element.13), channel_id=1, source_target_pairs={{0,6},{1,7},{2,0},{3,1},{4,2},{5,3},{6,4},{7,5},{8,14},{9,15},{10,... | collective-permute-start | bytes 110600 | tf_op jit(solution)/shard_map/ppermute | solution.py:60
  121.5 11.0 %collective-permute-start.15 = (f32[36,1024]{1,0:T(8,128)S(1)}, f32[36,1024]{1,0:T(8,128)S(1)}, u32[]{:S(2)}, u32[]{:S(2)}) collective-permute-start(f32[36,1024]{1,0:T(8,128)S(1)} %reshape.117), channel_id=1, source_target_pairs={{0,96},{8,104},{16,112},{24,120},{32,0},{40,8},{48,16},{56,24},{64... | collective-permute-start | bytes 442376 | tf_op jit(solution)/shard_map/ppermute | solution.py:60
  125.3 7.2 %collective-permute-start.14 = (f32[36,1024]{1,0:T(8,128)S(1)}, f32[36,1024]{1,0:T(8,128)S(1)}, u32[]{:S(2)}, u32[]{:S(2)}) collective-permute-start(f32[36,1024]{1,0:T(8,128)S(1)} %reshape.117), channel_id=1, source_target_pairs={{0,64},{8,72},{16,80},{24,88},{32,96},{40,104},{48,112},{56,120},{... | collective-permute-start | bytes 442376 | tf_op jit(solution)/shard_map/ppermute | solution.py:60
  125.3 7.1 %collective-permute-start.13 = (f32[36,1024]{1,0:T(8,128)S(1)}, f32[36,1024]{1,0:T(8,128)S(1)}, u32[]{:S(2)}, u32[]{:S(2)}) collective-permute-start(f32[36,1024]{1,0:T(8,128)S(1)} %reshape.117), channel_id=1, source_target_pairs={{0,32},{8,40},{16,48},{24,56},{32,64},{40,72},{48,80},{56,88},{64,... | collective-permute-start | bytes 442376 | tf_op jit(solution)/shard_map/ppermute | solution.py:60
  132.6 10.8 %collective-permute-start.16 = (f32[144,1024]{1,0:T(8,128)S(1)}, f32[144,1024]{1,0:T(8,128)S(1)}, u32[]{:S(2)}, u32[]{:S(2)}) collective-permute-start(f32[144,1024]{1,0:T(8,128)S(1)} %reshape.118), channel_id=1, source_target_pairs={{0,8},{8,16},{16,24},{24,0},{32,40},{40,48},{48,56},{56,32},{64,72... | collective-permute-start | bytes 1769480 | tf_op jit(solution)/shard_map/ppermute | solution.py:60
  134.0 23.1 %collective-permute-start.17 = (f32[144,1024]{1,0:T(8,128)S(1)}, f32[144,1024]{1,0:T(8,128)S(1)}, u32[]{:S(2)}, u32[]{:S(2)}) collective-permute-start(f32[144,1024]{1,0:T(8,128)S(1)} %reshape.118), channel_id=1, source_target_pairs={{0,16},{8,24},{16,0},{24,8},{32,48},{40,56},{48,32},{56,40},{64,80... | collective-permute-start | bytes 1769480 | tf_op jit(solution)/shard_map/ppermute | solution.py:60
  136.7 23.9 %collective-permute-start.18 = (f32[144,1024]{1,0:T(8,128)S(1)}, f32[144,1024]{1,0:T(8,128)S(1)}, u32[]{:S(2)}, u32[]{:S(2)}) collective-permute-start(f32[144,1024]{1,0:T(8,128)S(1)} %reshape.118), channel_id=1, source_target_pairs={{0,24},{8,0},{16,8},{24,16},{32,56},{40,32},{48,40},{56,48},{64,88... | collective-permute-start | bytes 1769480 | tf_op jit(solution)/shard_map/ppermute | solution.py:60
  161.5 28.4 %collective-permute-start.19 = (f32[576,1024]{1,0:T(8,128)}, f32[576,1024]{1,0:T(8,128)}, u32[]{:S(2)}, u32[]{:S(2)}) collective-permute-start(f32[576,1024]{1,0:T(8,128)} %bitcast.38), channel_id=1, source_target_pairs={{0,1},{1,0},{2,3},{3,2},{4,5},{5,4},{6,7},{7,6},{8,9},{9,8},{10,11... | collective-permute-start | bytes 7077896 | tf_op jit(solution)/shard_map/ppermute | solution.py:53
  177.8 54.0 %all-to-all-start.2 = ((bf16[8,256,1024]{2,1,0:T(8,128)(2,1)}), bf16[8,256,1024]{2,1,0:T(8,128)(2,1)}, u32[]{:S(2)}, u32[]{:S(2)}) async-start(bf16[8,256,1024]{2,1,0:T(8,128)(2,1)} %get-tuple-element.8), calls=%async_computation.2 | async-start | bytes 8388608 | tf_op jit(solution)/shard_map/all_to_all | solution.py:123
  187.6 4.3 %copy-start.4 = (f32[1024,1024]{1,0:T(8,128)S(1)}, f32[1024,1024]{1,0:T(8,128)}, u32[]{:S(2)}) copy-start(f32[1024,1024]{1,0:T(8,128)} %param.7) | copy-start | bytes 12582916
  193.8 2.0 copy-start.5
  239.6 24.4 %copy-start.8 = (bf16[1024,1024]{1,0:T(8,128)(2,1)S(1)}, bf16[1024,1024]{1,0:T(8,128)(2,1)}, u32[]{:S(2)}) copy-start(bf16[1024,1024]{1,0:T(8,128)(2,1)} %param.11) | copy-start | bytes 6291460
  264.0 14.9 %copy-start.1 = (bf16[1024,1024]{1,0:T(8,128)(2,1)S(1)}, bf16[1024,1024]{1,0:T(8,128)(2,1)}, u32[]{:S(2)}) copy-start(bf16[1024,1024]{1,0:T(8,128)(2,1)} %param.6) | copy-start | bytes 6291460

commit v2 on v0

--- a/solution.py
+++ b/solution.py
@@ -100,24 +100,23 @@
     )
     packed = lax.dynamic_update_slice(packed, part_counts.reshape(1, width), (clusters, 0))
     total = _all_sum(packed)
-    packed, x, labels = lax.optimization_barrier((packed, x, labels))
 
-    owner_group = jnp.take(partition_holder_team, labels, axis=0, mode="clip")
-    onehot = (owner_group[:, None] == jnp.arange(groups, dtype=jnp.int32)[None, :]).astype(jnp.int32)
-    before = jnp.cumsum(onehot, axis=0) - onehot
-    rank_in_group = jnp.sum(before * onehot, axis=1)
-    slot_index = owner_group * CAP + rank_in_group
-    source_row = (
-        jnp.zeros((groups * CAP,), jnp.int32).at[slot_index].set(jnp.arange(rows, dtype=jnp.int32))
+    every_x = lax.all_gather(x, "owners", axis=0, tiled=False)
+    every_label = lax.all_gather(labels, "owners", axis=0, tiled=False)
+    me = lax.axis_index("owners")
+    mine = jnp.take(partition_holder_team, every_label, axis=0, mode="clip") == me
+    mine_i = mine.astype(jnp.int32)
+    rank_in_group = jnp.cumsum(mine_i, axis=1) - mine_i
+    sources = jnp.broadcast_to(jnp.arange(groups, dtype=jnp.int32)[:, None], mine.shape)
+    slot_index = jnp.where(mine, sources * CAP + rank_in_group, groups * CAP)
+    row_of = jnp.broadcast_to(jnp.arange(rows, dtype=jnp.int32)[None, :], mine.shape) + sources * rows
+    source_row = jnp.zeros((groups * CAP,), jnp.int32).at[slot_index.reshape(-1)].set(
+        row_of.reshape(-1), mode="drop"
     )
-    slot_label = jnp.full((groups * CAP,), -1, jnp.int32).at[slot_index].set(labels)
-    slot_x = jnp.take(x, source_row, axis=0, mode="clip")
-    recv_x = lax.all_to_all(
-        slot_x.reshape(groups, CAP, width), "owners", split_axis=0, concat_axis=0, tiled=True
-    ).reshape(groups * CAP, width)
-    recv_label = lax.all_to_all(
-        slot_label.reshape(groups, CAP), "owners", split_axis=0, concat_axis=0, tiled=True
-    ).reshape(groups * CAP)
+    recv_label = jnp.full((groups * CAP,), -1, jnp.int32).at[slot_index.reshape(-1)].set(
+        every_label.reshape(-1), mode="drop"
+    )
+    recv_x = jnp.take(every_x.reshape(groups * rows, width), source_row, axis=0, mode="clip")
 
     valid = recv_label >= 0
     chooser = (recv_label[:, None] == jnp.arange(clusters, dtype=jnp.int32)[None, :]).astype(

time: 287 us -> 336 us (1.17)
  local copies, waits for them, and re-layouts: 47 us -> 149 us
  waiting for transfers between devices: 135 us -> 60.5 us
  blocking collectives: 0 us -> 15.9 us
  between operations: 1.85 us -> 15.1 us
  starting transfers between devices: 38.2 us -> 26 us
    ppermute x9, waiting for transfers between devices: 102 us -> 28.9 us  [_scatter_sum(): acc = acc + lax.ppermute(piece, name, perm)]
    scatter x2, local copies, waits for them, and re-layouts: 9.21 us -> 61.1 us  [the longest x1 30.7 us: shards(): jnp.zeros((groups * CAP,), jnp.int32).at[slot_index.reshape(-1)]]
    gather x2, local copies, waits for them, and re-layouts: 22.7 us -> 61.6 us  [the longest x1 32.9 us: shards(): jnp.take(partition_holder_team, every_label, axis=0, mode='clip') == me]
    all_gather x0 -> x1, blocking collectives: none -> 15.9 us  [shards(): every_label = lax.all_gather(labels, 'owners', axis=0, tiled=False)]
    all_to_all x2 -> x0, starting transfers between devices: 11.9 us -> none  [the longest x1 6.71 us: shards(): lax.all_to_all(slot_x.reshape(groups, CAP, width), 'owners', split_axis=0...]
    ppermute x9, waiting for transfers between devices: 33.4 us -> 26.4 us  [_gather(): lax.ppermute(d, name, perm)]
    dynamic_update_slice x9, local copies, waits for them, and re-layouts: 0.23 us -> 4.8 us  [_gather(): lax.dynamic_update_index_in_dim(out, lax.ppermute(d, name, perm), (me - s...]
    ppermute x1, waiting for transfers between devices: 0.01 us -> 4.5 us  [_scatter_sum(): return mine + lax.ppermute(other, 'owners', _CORES)]
  transfers between devices with their start and end apart: 22 -> 21, of which waited for: 11 -> 11; matrix products, arithmetic and copies ran while one was open for 16% -> 43% of each run, Pallas kernels for 0% -> 0%
where the time goes in v2:
time: 336 us; the launch traced here: 335 us
  local copies, waits for them, and re-layouts  149 us (44%)
  waiting for transfers between devices  60.5 us (18%)
  matrix products  47.8 us (14%)
  starting transfers between devices  26 us (8%)
  other arithmetic  20.6 us (6%)
  blocking collectives  15.9 us (5%)
  between operations  15.1 us (4%)
    gather x1, local copies, waits for them, and re-layouts, shards(): jnp.take(partition_holder_team, every_label, axis=0, mode='clip') == me  32.9 us
    scatter x1, local copies, waits for them, and re-layouts, shards(): jnp.zeros((groups * CAP,), jnp.int32).at[slot_index.reshape(-1)]  30.7 us
    scatter x1, local copies, waits for them, and re-layouts, shards(): jnp.full((groups * CAP,), -1, jnp.int32).at[slot_index.reshape(-1)]  30.5 us
    ppermute x9, waiting for transfers between devices, _scatter_sum(): acc = acc + lax.ppermute(piece, name, perm)  28.9 us
    gather x1, local copies, waits for them, and re-layouts, shards(): jnp.take(every_x.reshape(groups * rows, width), source_row, axis=0, mode=...  28.7 us
    ppermute x9, waiting for transfers between devices, _gather(): lax.ppermute(d, name, perm)  26.4 us
    dot_general x1, matrix products, shards(): jnp.dot(chooser, jnp.concatenate([high.astype(jnp.bfloat16), low], axis=0...  24.8 us
    all_gather x1, blocking collectives, shards(): every_label = lax.all_gather(labels, 'owners', axis=0, tiled=False)  15.9 us
  transfers between devices with their start and end apart: 21, of which 11 were waited for; matrix products, arithmetic and copies ran while one was open for 43% of the time, Pallas kernels for 0%

profile of v2, /device:TPU:1, one launch (start us, length us, event | category | flops | bytes accessed | tf_op | source)
XLA Modules:
  0.0 335.2 jit_solution(1027439852102259982)
XLA Ops:
  8.6 2.7 multiply_reduce_fusion
  12.0 4.0 %fusion.53 = (f32[1024]{0:T(1024)S(1)}, f32[1024,1024]{0,1:T(8,128)S(1)}) fusion(f32[]{:T(128)} %bitcast.93, f32[1024]{0:T(1024)S(1)} %multiply_reduce_fusion, bf16[1024,1024]{1,0:T(8,128)(2,1)} %param.6, f32[1024,1024]{1,0:T(8,128)S(1)} %copy-done.2), kind=kOutput, calls=%fused_computation.94 | convolution fusion | flops 2152725504 | bytes 10493956 | tf_op jit(solution)/shard_map/dot_general | solution.py:89
  18.2 4.2 %fusion.27 = f32[1152,1024]{1,0:T(8,128)} fusion(bf16[1024,1024]{1,0:T(8,128)(2,1)S(1)} %copy-done.6, bf16[1024,1024]{0,1:T(8,128)(2,1)S(1)} %get-tuple-element.9), kind=kOutput, calls=%fused_computation.32 | convolution fusion | flops 2415919104 | bytes 8912896 | tf_op jit(solution)/shard_map/dot_general | solution.py:98
  22.4 1.4 dynamic_update_slice.49
  23.8 3.9 %dynamic-slice_bitcast_fusion = f32[576,1024]{1,0:T(8,128)} fusion(f32[2,576,1024]{2,1,0:T(8,128)} %bitcast.100, s32[]{:T(128)S(6)} %select_n.209), kind=kLoop, calls=%fused_computation.31 | loop fusion | bytes 4718596 | tf_op jit(solution)/shard_map/jit(dynamic_index_in_dim)/squeeze | solution.py:36
  28.8 4.5 %collective-permute-done = f32[576,1024]{1,0:T(8,128)} collective-permute-done((f32[576,1024]{1,0:T(8,128)}, f32[576,1024]{1,0:T(8,128)}, u32[]{:S(2)}, u32[]{:S(2)}) %collective-permute-start) | collective-permute-done | bytes 2359328 | tf_op jit(solution)/shard_map/ppermute | solution.py:37
  33.3 3.1 bitcast_add_fusion
  36.4 1.4 copy-done.5
  37.8 1.2 dynamic-slice_bitcast_fusion.3
  39.0 1.4 collective-permute-start.1
  40.4 1.4 collective-permute-start.3
  41.8 1.6 collective-permute-start.2
  43.4 12.1 %collective-permute-done.1 = f32[144,1024]{1,0:T(8,128)S(1)} collective-permute-done((f32[144,1024]{1,0:T(8,128)}, f32[144,1024]{1,0:T(8,128)S(1)}, u32[]{:S(2)}, u32[]{:S(2)}) %collective-permute-start.1) | collective-permute-done | bytes 589856 | tf_op jit(solution)/shard_map/ppermute | solution.py:44
  56.3 12.7 %collective-permute-done.2 = f32[144,1024]{1,0:T(8,128)} collective-permute-done((f32[144,1024]{1,0:T(8,128)S(1)}, f32[144,1024]{1,0:T(8,128)}, u32[]{:S(2)}, u32[]{:S(2)}) %collective-permute-start.2) | collective-permute-done | bytes 589856 | tf_op jit(solution)/shard_map/ppermute | solution.py:44
  69.0 1.8 fusion.33
  71.6 1.7 collective-permute-start.4
  73.3 2.6 collective-permute-start.6
  75.9 1.2 collective-permute-start.5
  77.1 15.9 %all-gather = s32[8192]{0:T(1024)S(1)} all-gather(s32[1024]{0:T(1024)S(1)} %copy-done.8), channel_id=2, replica_groups=mesh['rows'=16,'owners'=8] {'owners'}, dimensions={0}, use_global_device_ids=true | all-gather | bytes 36864 | tf_op jit(solution)/shard_map/all_gather | solution.py:105
  95.0 1.9 collective-permute-start.9
  97.4 1.5 collective-permute-done.7
  98.8 2.6 collective-permute-done.8
  101.7 2.0 collective-permute-start.11
  104.2 2.3 collective-permute-done.10
  108.4 32.9 %gather_fusion = s32[8192]{0:T(1024)S(1)} fusion(s32[1024]{0:T(1024)S(1)} %copy-done.1, s32[8192]{0:T(1024)S(1)} %broadcast_clamp_fusion), kind=kCustom, calls=%fused_computation | custom fusion | bytes 98304 | tf_op jit(solution)/shard_map/jit(_take)/gather | solution.py:107
  141.3 1.9 collective-permute-start.15
  143.8 5.2 %collective-permute-done.14 = f32[36,1024]{1,0:T(8,128)S(1)} collective-permute-done((f32[36,1024]{1,0:T(8,128)S(1)}, f32[36,1024]{1,0:T(8,128)S(1)}, u32[]{:S(2)}, u32[]{:S(2)}) %collective-permute-start.14) | collective-permute-done | bytes 147488 | tf_op jit(solution)/shard_map/ppermute | solution.py:60
  150.7 2.3 reduce-window.6
  153.4 1.9 collective-permute-start.17
  155.4 1.4 collective-permute-start.18
  156.8 1.7 broadcast_in_dim.119
  159.4 2.0 collective-permute-done.16
  161.3 1.9 bitcast_dynamic-update-slice_fusion.4
  163.3 10.6 %collective-permute-done.17 = f32[144,1024]{1,0:T(8,128)} collective-permute-done((f32[144,1024]{1,0:T(8,128)}, f32[144,1024]{1,0:T(8,128)}, u32[]{:S(2)}, u32[]{:S(2)}) %collective-permute-start.17) | collective-permute-done | bytes 589856 | tf_op jit(solution)/shard_map/ppermute | solution.py:60
  173.9 1.9 bitcast_dynamic-update-slice_fusion.3
  175.8 5.8 %collective-permute-done.18 = f32[144,1024]{1,0:T(8,128)S(1)} collective-permute-done((f32[144,1024]{1,0:T(8,128)}, f32[144,1024]{1,0:T(8,128)S(1)}, u32[]{:S(2)}, u32[]{:S(2)}) %collective-permute-start.18) | collective-permute-done | bytes 589856 | tf_op jit(solution)/shard_map/ppermute | solution.py:60
  182.5 1.4 collective-permute-start.19
  184.1 30.5 %scatter_custom_fusion = s32[4096]{0:T(1024)S(1)} fusion(s32[8192]{0:T(1024)S(1)} %bitcast.104, s32[8192]{0:T(1024)S(1)} %all-gather, s32[]{:T(128)} %constant.231.clone.1), kind=kCustom, calls=%fused_computation.82 | custom fusion | bytes 16388 | tf_op jit(solution)/shard_map/scatter | solution.py:116
  214.6 30.7 %scatter_custom_fusion.1 = s32[4096]{0:T(1024)S(1)} fusion(s32[8192]{0:T(1024)S(1)} %bitcast.105, s32[8192]{0:T(1024)S(1)} %bitcast.106, s32[]{:T(128)} %constant.234.clone.1), kind=kCustom, calls=%fused_computation.79 | custom fusion | bytes 16388 | tf_op jit(solution)/shard_map/scatter | solution.py:113
  245.3 4.0 %iota_compare_fusion = pred[4096,1024]{1,0:T(32,128)(4,1)} fusion(s32[4096]{0:T(1024)S(1)} %scatter_custom_fusion), kind=kLoop, calls=%fused_computation.9 | loop fusion | flops 4194304 | bytes 4210688 | tf_op jit(solution)/shard_map/eq | solution.py:122
  249.9 2.2 bitcast_dynamic-update-slice_fusion.1
  252.1 2.0 bitcast_dynamic-update-slice_fusion
  254.1 1.9 reduce-precision_convert_fusion
  256.0 2.0 copy-done.4
  258.0 2.0 fusion.16
  260.1 28.7 %gather_fusion.1 = bf16[4096,1024]{1,0:T(8,128)(2,1)} fusion(bf16[8192,1024]{1,0:T(8,128)(2,1)} %all-gather.4.cloned.1.call-done, s32[4096]{0:T(1024)S(1)} %broadcast_clamp_fusion.1), kind=kCustom, calls=%fused_computation.1 | custom fusion | bytes 16793600 | tf_op jit(solution)/shard_map/jit(_take)/gather | solution.py:119
  288.8 24.8 %fusion.66 = bf16[4096,1024]{1,0:T(8,128)(2,1)} fusion(pred[4096]{0:T(1024)(128)(4,1)S(1)} %broadcast_compare_fusion.1, pred[4096,1024]{1,0:T(32,128)(4,1)} %iota_compare_fusion, bf16[4096,1024]{1,0:T(8,128)(2,1)} %gather_fusion.1, bf16[1024,1024]{1,0:T(8,128)(2,1)} %fusion.16, bf16[1024,1024]{1,0:T(8,128)(2,1)} %get-tuple-element.2), kind=kOutput, calls=%fused_computation.11.clone.clone.clone.1 | convolution fusion | flops 17213423616 | bytes 25169920 | tf_op jit(solution)/shard_map/dot_general | solution.py:134
  313.6 14.8 %fusion.9 = bf16[4096,1024]{1,0:T(8,128)(2,1)} fusion(bf16[1024,1024]{1,0:T(8,128)(2,1)S(1)} %copy-done, bf16[4096,1024]{1,0:T(8,128)(2,1)} %fusion.66), kind=kOutput, calls=%fused_computation.13 | convolution fusion | flops 8594128896 | bytes 18874368 | tf_op jit(solution)/shard_map/dot_general | solution.py:141
  (76 shorter events, 16.6 us)
Async XLA Ops:
  7.2 306.4 %copy-start = (bf16[1024,1024]{1,0:T(8,128)(2,1)S(1)}, bf16[1024,1024]{1,0:T(8,128)(2,1)}, u32[]{:S(2)}) copy-start(bf16[1024,1024]{1,0:T(8,128)(2,1)} %param.11) | copy-start | bytes 6291460
  7.2 252.9 %all-gather.4.cloned.1.call-start = ((), (), s32[]{:S(2)}) async-start(), calls=%async_computation | async-start | bytes 18874368 | tf_op jit(solution)/shard_map/all_gather | solution.py:104
  8.6 3.5 %copy-start.2 = (f32[1024,1024]{1,0:T(8,128)S(1)}, f32[1024,1024]{1,0:T(8,128)}, u32[]{:S(2)}) copy-start(f32[1024,1024]{1,0:T(8,128)} %param.7) | copy-start | bytes 12582916
  16.7 1.6 copy-start.6
  27.7 5.6 %collective-permute-start = (f32[576,1024]{1,0:T(8,128)}, f32[576,1024]{1,0:T(8,128)}, u32[]{:S(2)}, u32[]{:S(2)}) collective-permute-start(f32[576,1024]{1,0:T(8,128)} %dynamic-slice_bitcast_fusion), channel_id=1, source_target_pairs={{0,1},{1,0},{2,3},{3,2},{4,5},{5,4},{6,7},{7,6},{8,9},{9,8},{10,11... | collective-permute-start | bytes 7077896 | tf_op jit(solution)/shard_map/ppermute | solution.py:37
  36.4 1.4 copy-start.5
  37.8 39.3 %copy-start.8 = (s32[1024]{0:T(1024)S(1)}, s32[1024]{0:T(1024)}, u32[]{:S(2)}) copy-start(s32[1024]{0:T(1024)} %param.9) | copy-start | bytes 12292
  39.0 16.5 %collective-permute-start.1 = (f32[144,1024]{1,0:T(8,128)}, f32[144,1024]{1,0:T(8,128)S(1)}, u32[]{:S(2)}, u32[]{:S(2)}) collective-permute-start(f32[144,1024]{1,0:T(8,128)} %get-tuple-element.10), channel_id=1, source_target_pairs={{0,8},{8,16},{16,24},{24,0},{32,40},{40,48},{48,56},{56,32},{64,72... | collective-permute-start | bytes 1769480 | tf_op jit(solution)/shard_map/ppermute | solution.py:44
  40.4 15.1 %collective-permute-start.3 = (f32[144,1024]{1,0:T(8,128)}, f32[144,1024]{1,0:T(8,128)}, u32[]{:S(2)}, u32[]{:S(2)}) collective-permute-start(f32[144,1024]{1,0:T(8,128)} %get-tuple-element.11), channel_id=1, source_target_pairs={{0,24},{8,0},{16,8},{24,16},{32,56},{40,32},{48,40},{56,48},{64,88... | collective-permute-start | bytes 1769480 | tf_op jit(solution)/shard_map/ppermute | solution.py:44
  41.8 27.2 %collective-permute-start.2 = (f32[144,1024]{1,0:T(8,128)S(1)}, f32[144,1024]{1,0:T(8,128)}, u32[]{:S(2)}, u32[]{:S(2)}) collective-permute-start(f32[144,1024]{1,0:T(8,128)S(1)} %get-tuple-element.12), channel_id=1, source_target_pairs={{0,16},{8,24},{16,0},{24,8},{32,48},{40,56},{48,32},{56,40},{64,80... | collective-permute-start | bytes 1769480 | tf_op jit(solution)/shard_map/ppermute | solution.py:44
  43.4 65.0 %copy-start.1 = (s32[1024]{0:T(1024)S(1)}, s32[1024]{0:T(1024)}, u32[]{:S(2)}) copy-start(s32[1024]{0:T(1024)} %param.10) | copy-start | bytes 12292
  55.5 0.8 copy-start.7
  71.6 21.4 %collective-permute-start.4 = (f32[36,1024]{1,0:T(8,128)}, f32[36,1024]{1,0:T(8,128)S(1)}, u32[]{:S(2)}, u32[]{:S(2)}) collective-permute-start(f32[36,1024]{1,0:T(8,128)} %get-tuple-element.13), channel_id=1, source_target_pairs={{0,32},{8,40},{16,48},{24,56},{32,64},{40,72},{48,80},{56,88},{64,... | collective-permute-start | bytes 442376 | tf_op jit(solution)/shard_map/ppermute | solution.py:44
  73.3 19.7 %collective-permute-start.6 = (f32[36,1024]{1,0:T(8,128)S(1)}, f32[36,1024]{1,0:T(8,128)S(1)}, u32[]{:S(2)}, u32[]{:S(2)}) collective-permute-start(f32[36,1024]{1,0:T(8,128)S(1)} %get-tuple-element.14), channel_id=1, source_target_pairs={{0,96},{8,104},{16,112},{24,120},{32,0},{40,8},{48,16},{56,24},{64... | collective-permute-start | bytes 442376 | tf_op jit(solution)/shard_map/ppermute | solution.py:44
  75.9 17.1 %collective-permute-start.5 = (f32[36,1024]{1,0:T(8,128)S(1)}, f32[36,1024]{1,0:T(8,128)}, u32[]{:S(2)}, u32[]{:S(2)}) collective-permute-start(f32[36,1024]{1,0:T(8,128)S(1)} %get-tuple-element.15), channel_id=1, source_target_pairs={{0,64},{8,72},{16,80},{24,88},{32,96},{40,104},{48,112},{56,120},{... | collective-permute-start | bytes 442376 | tf_op jit(solution)/shard_map/ppermute | solution.py:44
  94.1 4.8 %collective-permute-start.7 = (f32[9,1024]{1,0:T(8,128)S(1)}, f32[9,1024]{1,0:T(8,128)S(1)}, u32[]{:S(2)}, u32[]{:S(2)}) collective-permute-start(f32[9,1024]{1,0:T(8,128)S(1)} %get-tuple-element.16), channel_id=1, source_target_pairs={{0,2},{1,3},{2,4},{3,5},{4,6},{5,7},{6,0},{7,1},{8,10},{9,11},{10,... | collective-permute-start | bytes 110600 | tf_op jit(solution)/shard_map/ppermute | solution.py:44
  95.0 3.9 %collective-permute-start.9 = (f32[9,1024]{1,0:T(8,128)S(1)}, f32[9,1024]{1,0:T(8,128)S(1)}, u32[]{:S(2)}, u32[]{:S(2)}) collective-permute-start(f32[9,1024]{1,0:T(8,128)S(1)} %get-tuple-element.17), channel_id=1, source_target_pairs={{0,6},{1,7},{2,0},{3,1},{4,2},{5,3},{6,4},{7,5},{8,14},{9,15},{10,... | collective-permute-start | bytes 110600 | tf_op jit(solution)/shard_map/ppermute | solution.py:44
  96.8 4.6 %collective-permute-start.8 = (f32[9,1024]{1,0:T(8,128)S(1)}, f32[9,1024]{1,0:T(8,128)S(1)}, u32[]{:S(2)}, u32[]{:S(2)}) collective-permute-start(f32[9,1024]{1,0:T(8,128)S(1)} %get-tuple-element.18), channel_id=1, source_target_pairs={{0,4},{1,5},{2,6},{3,7},{4,0},{5,1},{6,2},{7,3},{8,12},{9,13},{10,... | collective-permute-start | bytes 110600 | tf_op jit(solution)/shard_map/ppermute | solution.py:44
  101.5 5.1 %collective-permute-start.10 = (f32[9,1024]{1,0:T(8,128)S(1)}, f32[9,1024]{1,0:T(8,128)S(1)}, u32[]{:S(2)}, u32[]{:S(2)}) collective-permute-start(f32[9,1024]{1,0:T(8,128)S(1)} %get-tuple-element.5), channel_id=1, source_target_pairs={{0,2},{1,3},{2,4},{3,5},{4,6},{5,7},{6,0},{7,1},{8,10},{9,11},{10,... | collective-permute-start | bytes 110600 | tf_op jit(solution)/shard_map/ppermute | solution.py:60
  101.7 5.0 %collective-permute-start.11 = (f32[9,1024]{1,0:T(8,128)S(1)}, f32[9,1024]{1,0:T(8,128)S(1)}, u32[]{:S(2)}, u32[]{:S(2)}) collective-permute-start(f32[9,1024]{1,0:T(8,128)S(1)} %get-tuple-element.5), channel_id=1, source_target_pairs={{0,4},{1,5},{2,6},{3,7},{4,0},{5,1},{6,2},{7,3},{8,12},{9,13},{10,... | collective-permute-start | bytes 110600 | tf_op jit(solution)/shard_map/ppermute | solution.py:60
  103.7 3.5 %collective-permute-start.12 = (f32[9,1024]{1,0:T(8,128)S(1)}, f32[9,1024]{1,0:T(8,128)S(1)}, u32[]{:S(2)}, u32[]{:S(2)}) collective-permute-start(f32[9,1024]{1,0:T(8,128)S(1)} %get-tuple-element.5), channel_id=1, source_target_pairs={{0,6},{1,7},{2,0},{3,1},{4,2},{5,3},{6,4},{7,5},{8,14},{9,15},{10,... | collective-permute-start | bytes 110600 | tf_op jit(solution)/shard_map/ppermute | solution.py:60
  107.2 36.5 %collective-permute-start.13 = (f32[36,1024]{1,0:T(8,128)S(1)}, f32[36,1024]{1,0:T(8,128)S(1)}, u32[]{:S(2)}, u32[]{:S(2)}) collective-permute-start(f32[36,1024]{1,0:T(8,128)S(1)} %reshape.144), channel_id=1, source_target_pairs={{0,32},{8,40},{16,48},{24,56},{32,64},{40,72},{48,80},{56,88},{64,... | collective-permute-start | bytes 442376 | tf_op jit(solution)/shard_map/ppermute | solution.py:60
  141.3 7.6 %collective-permute-start.15 = (f32[36,1024]{1,0:T(8,128)S(1)}, f32[36,1024]{1,0:T(8,128)S(1)}, u32[]{:S(2)}, u32[]{:S(2)}) collective-permute-start(f32[36,1024]{1,0:T(8,128)S(1)} %reshape.144), channel_id=1, source_target_pairs={{0,96},{8,104},{16,112},{24,120},{32,0},{40,8},{48,16},{56,24},{64... | collective-permute-start | bytes 442376 | tf_op jit(solution)/shard_map/ppermute | solution.py:60
  143.3 5.7 %collective-permute-start.14 = (f32[36,1024]{1,0:T(8,128)S(1)}, f32[36,1024]{1,0:T(8,128)S(1)}, u32[]{:S(2)}, u32[]{:S(2)}) collective-permute-start(f32[36,1024]{1,0:T(8,128)S(1)} %reshape.144), channel_id=1, source_target_pairs={{0,64},{8,72},{16,80},{24,88},{32,96},{40,104},{48,112},{56,120},{... | collective-permute-start | bytes 442376 | tf_op jit(solution)/shard_map/ppermute | solution.py:60
  149.9 11.5 %collective-permute-start.16 = (f32[144,1024]{1,0:T(8,128)}, f32[144,1024]{1,0:T(8,128)}, u32[]{:S(2)}, u32[]{:S(2)}) collective-permute-start(f32[144,1024]{1,0:T(8,128)} %reshape.145), channel_id=1, source_target_pairs={{0,8},{8,16},{16,24},{24,0},{32,40},{40,48},{48,56},{56,32},{64,72... | collective-permute-start | bytes 1769480 | tf_op jit(solution)/shard_map/ppermute | solution.py:60
  153.4 20.5 %collective-permute-start.17 = (f32[144,1024]{1,0:T(8,128)}, f32[144,1024]{1,0:T(8,128)}, u32[]{:S(2)}, u32[]{:S(2)}) collective-permute-start(f32[144,1024]{1,0:T(8,128)} %reshape.145), channel_id=1, source_target_pairs={{0,16},{8,24},{16,0},{24,8},{32,48},{40,56},{48,32},{56,40},{64,80... | collective-permute-start | bytes 1769480 | tf_op jit(solution)/shard_map/ppermute | solution.py:60
  155.4 26.2 %collective-permute-start.18 = (f32[144,1024]{1,0:T(8,128)}, f32[144,1024]{1,0:T(8,128)S(1)}, u32[]{:S(2)}, u32[]{:S(2)}) collective-permute-start(f32[144,1024]{1,0:T(8,128)} %reshape.145), channel_id=1, source_target_pairs={{0,24},{8,0},{16,8},{24,16},{32,56},{40,32},{48,40},{56,48},{64,88... | collective-permute-start | bytes 1769480 | tf_op jit(solution)/shard_map/ppermute | solution.py:60
  182.5 69.6 %collective-permute-start.19 = (f32[576,1024]{1,0:T(8,128)}, f32[576,1024]{1,0:T(8,128)}, u32[]{:S(2)}, u32[]{:S(2)}) collective-permute-start(f32[576,1024]{1,0:T(8,128)} %bitcast.32), channel_id=1, source_target_pairs={{0,1},{1,0},{2,3},{3,2},{4,5},{5,4},{6,7},{7,6},{8,9},{9,8},{10,11... | collective-permute-start | bytes 7077896 | tf_op jit(solution)/shard_map/ppermute | solution.py:53
  249.8 4.3 %copy-start.3 = (f32[1024,1024]{1,0:T(8,128)S(1)}, f32[1024,1024]{1,0:T(8,128)}, u32[]{:S(2)}) copy-start(f32[1024,1024]{1,0:T(8,128)} %param.7) | copy-start | bytes 12582916
  256.0 2.0 copy-start.4
Sparse Core Ops, SparseCore 0:
  9.7 88.5 all-gather.3

commit v3 on v0

--- a/solution.py
+++ b/solution.py
@@ -100,8 +100,8 @@
     )
     packed = lax.dynamic_update_slice(packed, part_counts.reshape(1, width), (clusters, 0))
     total = _all_sum(packed)
-    packed, x, labels = lax.optimization_barrier((packed, x, labels))
 
+    every_x = lax.all_gather(x, "owners", axis=0, tiled=True)
     owner_group = jnp.take(partition_holder_team, labels, axis=0, mode="clip")
     onehot = (owner_group[:, None] == jnp.arange(groups, dtype=jnp.int32)[None, :]).astype(jnp.int32)
     before = jnp.cumsum(onehot, axis=0) - onehot
@@ -111,13 +111,12 @@
         jnp.zeros((groups * CAP,), jnp.int32).at[slot_index].set(jnp.arange(rows, dtype=jnp.int32))
     )
     slot_label = jnp.full((groups * CAP,), -1, jnp.int32).at[slot_index].set(labels)
-    slot_x = jnp.take(x, source_row, axis=0, mode="clip")
-    recv_x = lax.all_to_all(
-        slot_x.reshape(groups, CAP, width), "owners", split_axis=0, concat_axis=0, tiled=True
-    ).reshape(groups * CAP, width)
-    recv_label = lax.all_to_all(
-        slot_label.reshape(groups, CAP), "owners", split_axis=0, concat_axis=0, tiled=True
-    ).reshape(groups * CAP)
+    tables = jnp.stack([source_row.reshape(groups, CAP), slot_label.reshape(groups, CAP)], axis=1)
+    tables = lax.all_to_all(tables, "owners", split_axis=0, concat_axis=0, tiled=True)
+    sender = jnp.arange(groups, dtype=jnp.int32)[:, None] * rows
+    recv_row = (tables[:, 0] + sender).reshape(groups * CAP)
+    recv_label = tables[:, 1].reshape(groups * CAP)
+    recv_x = jnp.take(every_x, recv_row, axis=0, mode="clip")
 
     valid = recv_label >= 0
     chooser = (recv_label[:, None] == jnp.arange(clusters, dtype=jnp.int32)[None, :]).astype(

time: 287 us -> 246 us (0.86)
  waiting for transfers between devices: 135 us -> 55.4 us
  local copies, waits for them, and re-layouts: 47 us -> 68.5 us
  between operations: 1.85 us -> 15.2 us
    ppermute x9, waiting for transfers between devices: 102 us -> 30.2 us  [_scatter_sum(): acc = acc + lax.ppermute(piece, name, perm)]
    ppermute x9, waiting for transfers between devices: 33.4 us -> 15.4 us  [_gather(): lax.ppermute(d, name, perm)]
    gather x1, local copies, waits for them, and re-layouts: 18.1 us -> 28.7 us  [shards(): recv_x = jnp.take(every_x, recv_row, axis=0, mode='clip')]
    all_to_all x2 -> x1, starting transfers between devices: 11.9 us -> 3.82 us  [shards(): lax.all_to_all(tables, 'owners', split_axis=0, concat_axis=0, tiled=True)]
    all_to_all x2 -> x1, waiting for transfers between devices: 0.01 us -> 4.62 us  [shards(): lax.all_to_all(tables, 'owners', split_axis=0, concat_axis=0, tiled=True)]
    dynamic_update_slice x9, local copies, waits for them, and re-layouts: 0.23 us -> 4.79 us  [_gather(): lax.dynamic_update_index_in_dim(out, lax.ppermute(d, name, perm), (me - s...]
    ppermute x1, waiting for transfers between devices: 0.01 us -> 4.5 us  [_scatter_sum(): return mine + lax.ppermute(other, 'owners', _CORES)]
    ppermute x1, starting transfers between devices: 1.63 us -> 6.11 us  [_gather(): lax.ppermute(d, 'owners', _CORES)]
  transfers between devices with their start and end apart: 22 -> 22, of which waited for: 11 -> 13; matrix products, arithmetic and copies ran while one was open for 16% -> 26% of each run, Pallas kernels for 0% -> 0%
where the time goes in v3:
time: 246 us; the launch traced here: 245 us
  local copies, waits for them, and re-layouts  68.5 us (28%)
  waiting for transfers between devices  55.4 us (23%)
  matrix products  47.8 us (19%)
  starting transfers between devices  37.3 us (15%)
  other arithmetic  21.1 us (9%)
  between operations  15.2 us (6%)
    ppermute x9, waiting for transfers between devices, _scatter_sum(): acc = acc + lax.ppermute(piece, name, perm)  30.2 us
    gather x1, local copies, waits for them, and re-layouts, shards(): recv_x = jnp.take(every_x, recv_row, axis=0, mode='clip')  28.7 us
    dot_general x1, matrix products, shards(): jnp.dot(chooser, jnp.concatenate([high.astype(jnp.bfloat16), low], axis=0...  24.8 us
    ppermute x9, waiting for transfers between devices, _gather(): lax.ppermute(d, name, perm)  15.4 us
    dot_general x1, matrix products, shards(): jnp.dot(residual_vectors, orthogonal_quantizer_turn, preferred_element_ty...  14.8 us
    ppermute x9, starting transfers between devices, _scatter_sum(): acc = acc + lax.ppermute(piece, name, perm)  14.7 us
    ppermute x9, starting transfers between devices, _gather(): lax.ppermute(d, name, perm)  11.5 us
    ppermute x1, starting transfers between devices, _gather(): lax.ppermute(d, 'owners', _CORES)  6.11 us
  transfers between devices with their start and end apart: 22, of which 13 were waited for; matrix products, arithmetic and copies ran while one was open for 26% of the time, Pallas kernels for 0%

profile of v3, /device:TPU:1, one launch (start us, length us, event | category | flops | bytes accessed | tf_op | source)
XLA Modules:
  0.0 245.2 jit_solution(11922214735869538651)
XLA Ops:
  8.6 2.7 %multiply_reduce_fusion = f32[1024]{0:T(1024)S(1)} fusion(f32[1024,1024]{1,0:T(8,128)} %param.7), kind=kLoop, calls=%fused_computation.25 | loop fusion | flops 2096128 | bytes 4198400 | tf_op jit(solution)/shard_map/reduce_sum | solution.py:88
  12.0 4.0 %fusion.56 = (f32[1024]{0:T(1024)S(1)}, f32[1024,1024]{0,1:T(8,128)S(1)}) fusion(f32[]{:T(128)} %bitcast.110, f32[1024]{0:T(1024)S(1)} %multiply_reduce_fusion, bf16[1024,1024]{1,0:T(8,128)(2,1)} %param.6, f32[1024,1024]{1,0:T(8,128)S(1)} %copy-done.2), kind=kOutput, calls=%fused_computation.95 | convolution fusion | flops 2152725504 | bytes 10493956 | tf_op jit(solution)/shard_map/dot_general | solution.py:89
  18.2 4.2 %fusion.27 = f32[1152,1024]{1,0:T(8,128)} fusion(bf16[1024,1024]{1,0:T(8,128)(2,1)S(1)} %copy-done.6, bf16[1024,1024]{0,1:T(8,128)(2,1)S(1)} %get-tuple-element.7), kind=kOutput, calls=%fused_computation.32 | convolution fusion | flops 2415919104 | bytes 8912896 | tf_op jit(solution)/shard_map/dot_general | solution.py:98
  22.4 1.4 dynamic_update_slice.49
  23.8 3.9 %dynamic-slice_bitcast_fusion = f32[576,1024]{1,0:T(8,128)} fusion(f32[2,576,1024]{2,1,0:T(8,128)} %bitcast.117, s32[]{:T(128)S(6)} %select_n.196), kind=kLoop, calls=%fused_computation.31 | loop fusion | bytes 4718596 | tf_op jit(solution)/shard_map/jit(dynamic_index_in_dim)/squeeze | solution.py:36
  28.8 4.5 %collective-permute-done = f32[576,1024]{1,0:T(8,128)} collective-permute-done((f32[576,1024]{1,0:T(8,128)}, f32[576,1024]{1,0:T(8,128)}, u32[]{:S(2)}, u32[]{:S(2)}) %collective-permute-start) | collective-permute-done | bytes 2359328 | tf_op jit(solution)/shard_map/ppermute | solution.py:37
  33.3 3.1 %bitcast_add_fusion = f32[576,1024]{1,0:T(8,128)S(1)} fusion(f32[576,1024]{1,0:T(8,128)} %collective-permute-done, f32[2,576,1024]{2,1,0:T(8,128)} %bitcast.118, s32[]{:T(128)S(6)} %select_n.195), kind=kLoop, calls=%fused_computation.30 | loop fusion | flops 589824 | bytes 7077892 | tf_op jit(solution)/shard_map/add | solution.py:37
  36.4 1.4 copy-done.5
  39.0 1.4 collective-permute-start.1
  40.4 1.4 collective-permute-start.3
  41.8 1.6 collective-permute-start.2
  43.4 12.1 %collective-permute-done.1 = f32[144,1024]{1,0:T(8,128)S(1)} collective-permute-done((f32[144,1024]{1,0:T(8,128)}, f32[144,1024]{1,0:T(8,128)S(1)}, u32[]{:S(2)}, u32[]{:S(2)}) %collective-permute-start.1) | collective-permute-done | bytes 589856 | tf_op jit(solution)/shard_map/ppermute | solution.py:44
  56.3 12.7 %collective-permute-done.2 = f32[144,1024]{1,0:T(8,128)} collective-permute-done((f32[144,1024]{1,0:T(8,128)S(1)}, f32[144,1024]{1,0:T(8,128)}, u32[]{:S(2)}, u32[]{:S(2)}) %collective-permute-start.2) | collective-permute-done | bytes 589856 | tf_op jit(solution)/shard_map/ppermute | solution.py:44
  69.0 1.8 fusion.33
  71.6 1.7 collective-permute-start.4
  73.4 2.6 %collective-permute-start.6 = (f32[36,1024]{1,0:T(8,128)S(1)}, f32[36,1024]{1,0:T(8,128)S(1)}, u32[]{:S(2)}, u32[]{:S(2)}) collective-permute-start(f32[36,1024]{1,0:T(8,128)S(1)} %get-tuple-element.12), channel_id=1, source_target_pairs={{0,96},{8,104},{16,112},{24,120},{32,0},{40,8},{48,16},{56,24},{64... | collective-permute-start | bytes 442376 | tf_op jit(solution)/shard_map/ppermute | solution.py:44
  77.1 4.5 %gather_fusion = s32[1024]{0:T(1024)S(1)} fusion(s32[1024]{0:T(1024)S(1)} %copy-done.1, s32[1024]{0:T(1024)S(1)} %broadcast_clamp_fusion.1), kind=kCustom, calls=%fused_computation | custom fusion | bytes 12288 | tf_op jit(solution)/shard_map/jit(_take)/gather | solution.py:105
  81.7 2.3 collective-permute-done.5
  85.0 1.8 collective-permute-start.7
  88.1 1.7 collective-permute-start.8
  89.8 2.3 reduce-window.6
  92.1 3.1 %collective-permute-done.8 = f32[9,1024]{1,0:T(8,128)S(1)} collective-permute-done((f32[9,1024]{1,0:T(8,128)S(1)}, f32[9,1024]{1,0:T(8,128)S(1)}, u32[]{:S(2)}, u32[]{:S(2)}) %collective-permute-start.8) | collective-permute-done | bytes 36896 | tf_op jit(solution)/shard_map/ppermute | solution.py:44
  96.5 1.8 collective-permute-start.11
  99.6 1.6 collective-permute-done.11
  102.0 2.5 %collective-permute-start.15 = (f32[36,1024]{1,0:T(8,128)S(1)}, f32[36,1024]{1,0:T(8,128)S(1)}, u32[]{:S(2)}, u32[]{:S(2)}) collective-permute-start(f32[36,1024]{1,0:T(8,128)S(1)} %reshape.127), channel_id=1, source_target_pairs={{0,96},{8,104},{16,112},{24,120},{32,0},{40,8},{48,16},{56,24},{64... | collective-permute-start | bytes 442376 | tf_op jit(solution)/shard_map/ppermute | solution.py:60
  105.1 2.0 collective-permute-done.13
  107.1 3.1 %collective-permute-done.14 = f32[36,1024]{1,0:T(8,128)S(1)} collective-permute-done((f32[36,1024]{1,0:T(8,128)S(1)}, f32[36,1024]{1,0:T(8,128)S(1)}, u32[]{:S(2)}, u32[]{:S(2)}) %collective-permute-start.14) | collective-permute-done | bytes 147488 | tf_op jit(solution)/shard_map/ppermute | solution.py:60
  111.3 2.5 %collective-permute-start.17 = (f32[144,1024]{1,0:T(8,128)}, f32[144,1024]{1,0:T(8,128)}, u32[]{:S(2)}, u32[]{:S(2)}) collective-permute-start(f32[144,1024]{1,0:T(8,128)} %reshape.128), channel_id=1, source_target_pairs={{0,16},{8,24},{16,0},{24,8},{32,48},{40,56},{48,32},{56,40},{64,80... | collective-permute-start | bytes 1769480 | tf_op jit(solution)/shard_map/ppermute | solution.py:60
  113.8 4.3 %scatter_custom_fusion.1 = s32[4096]{0:T(1024)S(1)} fusion(s32[1024]{0:T(1024)S(1)} %bitcast.131, s32[1024]{0:T(1024)S(1)} %copy-done.8, s32[]{:T(128)} %constant.234.clone.1), kind=kCustom, calls=%fused_computation.78 | custom fusion | bytes 16388 | tf_op jit(solution)/shard_map/scatter | solution.py:113
  118.2 4.3 %scatter_custom_fusion = s32[4096]{0:T(1024)S(1)} fusion(s32[1024]{0:T(1024)S(1)} %bitcast.132, s32[1024]{0:T(1024)S(1)} %iota.20, s32[]{:T(128)} %constant.231.clone.1), kind=kCustom, calls=%fused_computation.81 | custom fusion | bytes 16388 | tf_op jit(solution)/shard_map/scatter | solution.py:111
  122.6 2.0 collective-permute-start.18
  124.5 1.7 broadcast_in_dim.93
  127.1 1.9 bitcast_dynamic-update-slice_fusion.4
  129.0 4.5 %collective-permute-done.17 = f32[144,1024]{1,0:T(8,128)} collective-permute-done((f32[144,1024]{1,0:T(8,128)}, f32[144,1024]{1,0:T(8,128)}, u32[]{:S(2)}, u32[]{:S(2)}) %collective-permute-start.17) | collective-permute-done | bytes 589856 | tf_op jit(solution)/shard_map/ppermute | solution.py:60
  133.6 1.9 bitcast_dynamic-update-slice_fusion.3
  135.5 3.6 %collective-permute-done.18 = f32[144,1024]{1,0:T(8,128)S(1)} collective-permute-done((f32[144,1024]{1,0:T(8,128)}, f32[144,1024]{1,0:T(8,128)S(1)}, u32[]{:S(2)}, u32[]{:S(2)}) %collective-permute-start.18) | collective-permute-done | bytes 589856 | tf_op jit(solution)/shard_map/ppermute | solution.py:60
  139.9 6.1 %collective-permute-start.19 = (f32[576,1024]{1,0:T(8,128)}, f32[576,1024]{1,0:T(8,128)}, u32[]{:S(2)}, u32[]{:S(2)}) collective-permute-start(f32[576,1024]{1,0:T(8,128)} %bitcast.38), channel_id=1, source_target_pairs={{0,1},{1,0},{2,3},{3,2},{4,5},{5,4},{6,7},{7,6},{8,9},{9,8},{10,11... | collective-permute-start | bytes 7077896 | tf_op jit(solution)/shard_map/ppermute | solution.py:53
  146.7 3.8 %all-to-all-start = ((s32[8,2,512]{2,1,0:T(2,128)}), s32[8,2,512]{2,1,0:T(2,128)S(1)}, u32[]{:S(2)}, u32[]{:S(2)}) async-start(s32[8,2,512]{2,1,0:T(2,128)} %pad_add_fusion), calls=%async_computation | async-start | bytes 65536 | tf_op jit(solution)/shard_map/all_to_all | solution.py:115
  150.6 4.6 %all-to-all-done = s32[8,2,512]{2,1,0:T(2,128)S(1)} async-done(((s32[8,2,512]{2,1,0:T(2,128)}), s32[8,2,512]{2,1,0:T(2,128)S(1)}, u32[]{:S(2)}, u32[]{:S(2)}) %all-to-all-start) | async-done | bytes 32800 | tf_op jit(solution)/shard_map/all_to_all | solution.py:115
  155.3 4.0 %iota_compare_fusion = pred[4096,1024]{1,0:T(32,128)(4,1)} fusion(s32[4096]{0:T(1024)S(1)} %bitcast.120), kind=kLoop, calls=%fused_computation.9 | loop fusion | flops 4194304 | bytes 4210688 | tf_op jit(solution)/shard_map/eq | solution.py:122
  159.9 2.2 bitcast_dynamic-update-slice_fusion.1
  162.1 2.0 bitcast_dynamic-update-slice_fusion
  164.1 1.9 reduce-precision_convert_fusion
  166.0 2.0 copy-done.4
  168.0 2.1 fusion.16
  170.1 28.7 %gather_fusion.1 = bf16[4096,1024]{1,0:T(8,128)(2,1)} fusion(bf16[8192,1024]{1,0:T(8,128)(2,1)} %all-gather.2.cloned.1.call-done, s32[4096]{0:T(1024)S(1)} %broadcast_clamp_fusion), kind=kCustom, calls=%fused_computation.1 | custom fusion | bytes 16793600 | tf_op jit(solution)/shard_map/jit(_take)/gather | solution.py:119
  198.8 24.8 %fusion.69 = bf16[4096,1024]{1,0:T(8,128)(2,1)} fusion(pred[4096]{0:T(1024)(128)(4,1)S(1)} %broadcast_compare_fusion, pred[4096,1024]{1,0:T(32,128)(4,1)} %iota_compare_fusion, bf16[4096,1024]{1,0:T(8,128)(2,1)} %gather_fusion.1, bf16[1024,1024]{1,0:T(8,128)(2,1)} %fusion.16, bf16[1024,1024]{1,0:T(8,128)(2,1)} %get-tuple-element.2), kind=kOutput, calls=%fused_computation.11.clone.clone.clone.1 | convolution fusion | flops 17213423616 | bytes 25169920 | tf_op jit(solution)/shard_map/dot_general | solution.py:134
  223.6 14.8 %fusion.9 = bf16[4096,1024]{1,0:T(8,128)(2,1)} fusion(bf16[1024,1024]{1,0:T(8,128)(2,1)S(1)} %copy-done, bf16[4096,1024]{1,0:T(8,128)(2,1)} %fusion.69), kind=kOutput, calls=%fused_computation.13 | convolution fusion | flops 8594128896 | bytes 18874368 | tf_op jit(solution)/shard_map/dot_general | solution.py:141
  (80 shorter events, 19.2 us)
Async XLA Ops:
  7.2 216.4 %copy-start = (bf16[1024,1024]{1,0:T(8,128)(2,1)S(1)}, bf16[1024,1024]{1,0:T(8,128)(2,1)}, u32[]{:S(2)}) copy-start(bf16[1024,1024]{1,0:T(8,128)(2,1)} %param.11) | copy-start | bytes 6291460
  7.2 162.9 %all-gather.2.cloned.1.call-start = ((), (), s32[]{:S(2)}) async-start(), calls=%async_computation.1 | async-start | bytes 18874368 | tf_op jit(solution)/shard_map/all_gather | solution.py:104
  8.6 3.5 %copy-start.2 = (f32[1024,1024]{1,0:T(8,128)S(1)}, f32[1024,1024]{1,0:T(8,128)}, u32[]{:S(2)}) copy-start(f32[1024,1024]{1,0:T(8,128)} %param.7) | copy-start | bytes 12582916
  16.7 1.6 copy-start.6
  27.7 5.6 %collective-permute-start = (f32[576,1024]{1,0:T(8,128)}, f32[576,1024]{1,0:T(8,128)}, u32[]{:S(2)}, u32[]{:S(2)}) collective-permute-start(f32[576,1024]{1,0:T(8,128)} %dynamic-slice_bitcast_fusion), channel_id=1, source_target_pairs={{0,1},{1,0},{2,3},{3,2},{4,5},{5,4},{6,7},{7,6},{8,9},{9,8},{10,11... | collective-permute-start | bytes 7077896 | tf_op jit(solution)/shard_map/ppermute | solution.py:37
  36.4 1.4 copy-start.5
  37.8 39.3 %copy-start.8 = (s32[1024]{0:T(1024)S(1)}, s32[1024]{0:T(1024)}, u32[]{:S(2)}) copy-start(s32[1024]{0:T(1024)} %param.9) | copy-start | bytes 12292
  37.8 39.3 %copy-start.1 = (s32[1024]{0:T(1024)S(1)}, s32[1024]{0:T(1024)}, u32[]{:S(2)}) copy-start(s32[1024]{0:T(1024)} %param.10) | copy-start | bytes 12292
  39.0 16.5 %collective-permute-start.1 = (f32[144,1024]{1,0:T(8,128)}, f32[144,1024]{1,0:T(8,128)S(1)}, u32[]{:S(2)}, u32[]{:S(2)}) collective-permute-start(f32[144,1024]{1,0:T(8,128)} %get-tuple-element.8), channel_id=1, source_target_pairs={{0,8},{8,16},{16,24},{24,0},{32,40},{40,48},{48,56},{56,32},{64,72... | collective-permute-start | bytes 1769480 | tf_op jit(solution)/shard_map/ppermute | solution.py:44
  40.4 15.1 %collective-permute-start.3 = (f32[144,1024]{1,0:T(8,128)}, f32[144,1024]{1,0:T(8,128)}, u32[]{:S(2)}, u32[]{:S(2)}) collective-permute-start(f32[144,1024]{1,0:T(8,128)} %get-tuple-element.9), channel_id=1, source_target_pairs={{0,24},{8,0},{16,8},{24,16},{32,56},{40,32},{48,40},{56,48},{64,88... | collective-permute-start | bytes 1769480 | tf_op jit(solution)/shard_map/ppermute | solution.py:44
  41.8 27.2 %collective-permute-start.2 = (f32[144,1024]{1,0:T(8,128)S(1)}, f32[144,1024]{1,0:T(8,128)}, u32[]{:S(2)}, u32[]{:S(2)}) collective-permute-start(f32[144,1024]{1,0:T(8,128)S(1)} %get-tuple-element.10), channel_id=1, source_target_pairs={{0,16},{8,24},{16,0},{24,8},{32,48},{40,56},{48,32},{56,40},{64,80... | collective-permute-start | bytes 1769480 | tf_op jit(solution)/shard_map/ppermute | solution.py:44
  55.5 0.8 copy-start.7
  71.6 10.1 %collective-permute-start.4 = (f32[36,1024]{1,0:T(8,128)}, f32[36,1024]{1,0:T(8,128)S(1)}, u32[]{:S(2)}, u32[]{:S(2)}) collective-permute-start(f32[36,1024]{1,0:T(8,128)} %get-tuple-element.11), channel_id=1, source_target_pairs={{0,32},{8,40},{16,48},{24,56},{32,64},{40,72},{48,80},{56,88},{64,... | collective-permute-start | bytes 442376 | tf_op jit(solution)/shard_map/ppermute | solution.py:44
  73.4 8.3 %collective-permute-start.6 = (f32[36,1024]{1,0:T(8,128)S(1)}, f32[36,1024]{1,0:T(8,128)S(1)}, u32[]{:S(2)}, u32[]{:S(2)}) collective-permute-start(f32[36,1024]{1,0:T(8,128)S(1)} %get-tuple-element.12), channel_id=1, source_target_pairs={{0,96},{8,104},{16,112},{24,120},{32,0},{40,8},{48,16},{56,24},{64... | collective-permute-start | bytes 442376 | tf_op jit(solution)/shard_map/ppermute | solution.py:44
  75.9 8.1 %collective-permute-start.5 = (f32[36,1024]{1,0:T(8,128)S(1)}, f32[36,1024]{1,0:T(8,128)}, u32[]{:S(2)}, u32[]{:S(2)}) collective-permute-start(f32[36,1024]{1,0:T(8,128)S(1)} %get-tuple-element.13), channel_id=1, source_target_pairs={{0,64},{8,72},{16,80},{24,88},{32,96},{40,104},{48,112},{56,120},{... | collective-permute-start | bytes 442376 | tf_op jit(solution)/shard_map/ppermute | solution.py:44
  85.0 7.0 %collective-permute-start.7 = (f32[9,1024]{1,0:T(8,128)S(1)}, f32[9,1024]{1,0:T(8,128)S(1)}, u32[]{:S(2)}, u32[]{:S(2)}) collective-permute-start(f32[9,1024]{1,0:T(8,128)S(1)} %get-tuple-element.14), channel_id=1, source_target_pairs={{0,2},{1,3},{2,4},{3,5},{4,6},{5,7},{6,0},{7,1},{8,10},{9,11},{10,... | collective-permute-start | bytes 110600 | tf_op jit(solution)/shard_map/ppermute | solution.py:44
  86.8 5.3 %collective-permute-start.9 = (f32[9,1024]{1,0:T(8,128)S(1)}, f32[9,1024]{1,0:T(8,128)S(1)}, u32[]{:S(2)}, u32[]{:S(2)}) collective-permute-start(f32[9,1024]{1,0:T(8,128)S(1)} %get-tuple-element.15), channel_id=1, source_target_pairs={{0,6},{1,7},{2,0},{3,1},{4,2},{5,3},{6,4},{7,5},{8,14},{9,15},{10,... | collective-permute-start | bytes 110600 | tf_op jit(solution)/shard_map/ppermute | solution.py:44
  88.1 7.0 %collective-permute-start.8 = (f32[9,1024]{1,0:T(8,128)S(1)}, f32[9,1024]{1,0:T(8,128)S(1)}, u32[]{:S(2)}, u32[]{:S(2)}) collective-permute-start(f32[9,1024]{1,0:T(8,128)S(1)} %get-tuple-element.16), channel_id=1, source_target_pairs={{0,4},{1,5},{2,6},{3,7},{4,0},{5,1},{6,2},{7,3},{8,12},{9,13},{10,... | collective-permute-start | bytes 110600 | tf_op jit(solution)/shard_map/ppermute | solution.py:44
  95.2 4.4 %collective-permute-start.10 = (f32[9,1024]{1,0:T(8,128)S(1)}, f32[9,1024]{1,0:T(8,128)S(1)}, u32[]{:S(2)}, u32[]{:S(2)}) collective-permute-start(f32[9,1024]{1,0:T(8,128)S(1)} %get-tuple-element.5), channel_id=1, source_target_pairs={{0,2},{1,3},{2,4},{3,5},{4,6},{5,7},{6,0},{7,1},{8,10},{9,11},{10,... | collective-permute-start | bytes 110600 | tf_op jit(solution)/shard_map/ppermute | solution.py:60
  96.5 4.6 %collective-permute-start.11 = (f32[9,1024]{1,0:T(8,128)S(1)}, f32[9,1024]{1,0:T(8,128)S(1)}, u32[]{:S(2)}, u32[]{:S(2)}) collective-permute-start(f32[9,1024]{1,0:T(8,128)S(1)} %get-tuple-element.5), channel_id=1, source_target_pairs={{0,4},{1,5},{2,6},{3,7},{4,0},{5,1},{6,2},{7,3},{8,12},{9,13},{10,... | collective-permute-start | bytes 110600 | tf_op jit(solution)/shard_map/ppermute | solution.py:60
  98.3 3.1 %collective-permute-start.12 = (f32[9,1024]{1,0:T(8,128)S(1)}, f32[9,1024]{1,0:T(8,128)S(1)}, u32[]{:S(2)}, u32[]{:S(2)}) collective-permute-start(f32[9,1024]{1,0:T(8,128)S(1)} %get-tuple-element.5), channel_id=1, source_target_pairs={{0,6},{1,7},{2,0},{3,1},{4,2},{5,3},{6,4},{7,5},{8,14},{9,15},{10,... | collective-permute-start | bytes 110600 | tf_op jit(solution)/shard_map/ppermute | solution.py:60
  101.5 5.6 %collective-permute-start.13 = (f32[36,1024]{1,0:T(8,128)S(1)}, f32[36,1024]{1,0:T(8,128)S(1)}, u32[]{:S(2)}, u32[]{:S(2)}) collective-permute-start(f32[36,1024]{1,0:T(8,128)S(1)} %reshape.127), channel_id=1, source_target_pairs={{0,32},{8,40},{16,48},{24,56},{32,64},{40,72},{48,80},{56,88},{64,... | collective-permute-start | bytes 442376 | tf_op jit(solution)/shard_map/ppermute | solution.py:60
  102.0 8.2 %collective-permute-start.15 = (f32[36,1024]{1,0:T(8,128)S(1)}, f32[36,1024]{1,0:T(8,128)S(1)}, u32[]{:S(2)}, u32[]{:S(2)}) collective-permute-start(f32[36,1024]{1,0:T(8,128)S(1)} %reshape.127), channel_id=1, source_target_pairs={{0,96},{8,104},{16,112},{24,120},{32,0},{40,8},{48,16},{56,24},{64... | collective-permute-start | bytes 442376 | tf_op jit(solution)/shard_map/ppermute | solution.py:60
  104.6 5.7 %collective-permute-start.14 = (f32[36,1024]{1,0:T(8,128)S(1)}, f32[36,1024]{1,0:T(8,128)S(1)}, u32[]{:S(2)}, u32[]{:S(2)}) collective-permute-start(f32[36,1024]{1,0:T(8,128)S(1)} %reshape.127), channel_id=1, source_target_pairs={{0,64},{8,72},{16,80},{24,88},{32,96},{40,104},{48,112},{56,120},{... | collective-permute-start | bytes 442376 | tf_op jit(solution)/shard_map/ppermute | solution.py:60
  111.2 15.9 %collective-permute-start.16 = (f32[144,1024]{1,0:T(8,128)}, f32[144,1024]{1,0:T(8,128)}, u32[]{:S(2)}, u32[]{:S(2)}) collective-permute-start(f32[144,1024]{1,0:T(8,128)} %reshape.128), channel_id=1, source_target_pairs={{0,8},{8,16},{16,24},{24,0},{32,40},{40,48},{48,56},{56,32},{64,72... | collective-permute-start | bytes 1769480 | tf_op jit(solution)/shard_map/ppermute | solution.py:60
  111.3 22.3 %collective-permute-start.17 = (f32[144,1024]{1,0:T(8,128)}, f32[144,1024]{1,0:T(8,128)}, u32[]{:S(2)}, u32[]{:S(2)}) collective-permute-start(f32[144,1024]{1,0:T(8,128)} %reshape.128), channel_id=1, source_target_pairs={{0,16},{8,24},{16,0},{24,8},{32,48},{40,56},{48,32},{56,40},{64,80... | collective-permute-start | bytes 1769480 | tf_op jit(solution)/shard_map/ppermute | solution.py:60
  122.6 16.5 %collective-permute-start.18 = (f32[144,1024]{1,0:T(8,128)}, f32[144,1024]{1,0:T(8,128)S(1)}, u32[]{:S(2)}, u32[]{:S(2)}) collective-permute-start(f32[144,1024]{1,0:T(8,128)} %reshape.128), channel_id=1, source_target_pairs={{0,24},{8,0},{16,8},{24,16},{32,56},{40,32},{48,40},{56,48},{64,88... | collective-permute-start | bytes 1769480 | tf_op jit(solution)/shard_map/ppermute | solution.py:60
  139.9 22.1 %collective-permute-start.19 = (f32[576,1024]{1,0:T(8,128)}, f32[576,1024]{1,0:T(8,128)}, u32[]{:S(2)}, u32[]{:S(2)}) collective-permute-start(f32[576,1024]{1,0:T(8,128)} %bitcast.38), channel_id=1, source_target_pairs={{0,1},{1,0},{2,3},{3,2},{4,5},{5,4},{6,7},{7,6},{8,9},{9,8},{10,11... | collective-permute-start | bytes 7077896 | tf_op jit(solution)/shard_map/ppermute | solution.py:53
  146.7 8.5 %all-to-all-start = ((s32[8,2,512]{2,1,0:T(2,128)}), s32[8,2,512]{2,1,0:T(2,128)S(1)}, u32[]{:S(2)}, u32[]{:S(2)}) async-start(s32[8,2,512]{2,1,0:T(2,128)} %pad_add_fusion), calls=%async_computation | async-start | bytes 65536 | tf_op jit(solution)/shard_map/all_to_all | solution.py:115
  159.8 4.3 %copy-start.3 = (f32[1024,1024]{1,0:T(8,128)S(1)}, f32[1024,1024]{1,0:T(8,128)}, u32[]{:S(2)}) copy-start(f32[1024,1024]{1,0:T(8,128)} %param.7) | copy-start | bytes 12582916
  166.0 2.0 copy-start.4
Sparse Core Ops, SparseCore 0:
  9.7 91.2 all-gather.1

commit v4 on v3

--- a/solution.py
+++ b/solution.py
@@ -99,9 +99,13 @@
         weights_wide, x, (((0,), (0,)), ((), ())), preferred_element_type=jnp.float32
     )
     packed = lax.dynamic_update_slice(packed, part_counts.reshape(1, width), (clusters, 0))
-    total = _all_sum(packed)
+    partial = packed
+    for axis in ("core", "y", "z", "x"):
+        partial = _scatter_sum(partial, axis)
+    partial = _gather(partial, "x")
+    partial = _gather(partial, "z")
 
-    every_x = lax.all_gather(x, "owners", axis=0, tiled=True)
+    every_x = lax.all_gather(x, "owners", axis=0, tiled=False)
     owner_group = jnp.take(partition_holder_team, labels, axis=0, mode="clip")
     onehot = (owner_group[:, None] == jnp.arange(groups, dtype=jnp.int32)[None, :]).astype(jnp.int32)
     before = jnp.cumsum(onehot, axis=0) - onehot
@@ -113,10 +117,17 @@
     slot_label = jnp.full((groups * CAP,), -1, jnp.int32).at[slot_index].set(labels)
     tables = jnp.stack([source_row.reshape(groups, CAP), slot_label.reshape(groups, CAP)], axis=1)
     tables = lax.all_to_all(tables, "owners", split_axis=0, concat_axis=0, tiled=True)
-    sender = jnp.arange(groups, dtype=jnp.int32)[:, None] * rows
-    recv_row = (tables[:, 0] + sender).reshape(groups * CAP)
     recv_label = tables[:, 1].reshape(groups * CAP)
-    recv_x = jnp.take(every_x, recv_row, axis=0, mode="clip")
+    picker = (tables[:, 0][:, :, None] == jnp.arange(rows, dtype=jnp.int32)[None, None, :]).astype(
+        jnp.bfloat16
+    )
+    recv_x = jnp.einsum(
+        "sqn,snd->sqd", picker, every_x, preferred_element_type=jnp.float32
+    ).astype(jnp.bfloat16).reshape(groups * CAP, width)
+    partial, recv_x = lax.optimization_barrier((partial, recv_x))
+    for axis in ("y", "core"):
+        partial = _gather(partial, axis)
+    total = partial
 
     valid = recv_label >= 0
     chooser = (recv_label[:, None] == jnp.arange(clusters, dtype=jnp.int32)[None, :]).astype(

time: 246 us -> 228 us (0.927)
  local copies, waits for them, and re-layouts: 68.5 us -> 28.5 us
  matrix products: 47.8 us -> 64.8 us
  waiting for transfers between devices: 55.4 us -> 61.9 us
    gather x1 -> x0, local copies, waits for them, and re-layouts: 28.7 us -> none  [shards(): recv_x = jnp.take(every_x, recv_row, axis=0, mode='clip')]
    ppermute x9, waiting for transfers between devices: 15.4 us -> 32.5 us  [_gather(): lax.ppermute(d, name, perm)]
    dot_general x0 -> x1, matrix products: none -> 17 us  [shards(): jnp.einsum('sqn,snd->sqd', picker, every_x, preferred_element_type=jnp.fl...]
    all_to_all x1, waiting for transfers between devices: 4.62 us -> 0.01 us  [shards(): lax.all_to_all(tables, 'owners', split_axis=0, concat_axis=0, tiled=True)]
    ppermute x1, waiting for transfers between devices: 4.5 us -> 0.01 us  [_scatter_sum(): return mine + lax.ppermute(other, 'owners', _CORES)]
    ppermute x1, starting transfers between devices: 6.11 us -> 2.54 us  [_gather(): lax.ppermute(d, 'owners', _CORES)]
    dynamic_update_slice x9, local copies, waits for them, and re-layouts: 4.79 us -> 1.28 us  [_gather(): lax.dynamic_update_index_in_dim(out, lax.ppermute(d, name, perm), (me - s...]
    all_to_all x1, starting transfers between devices: 3.82 us -> 7.12 us  [shards(): lax.all_to_all(tables, 'owners', split_axis=0, concat_axis=0, tiled=True)]
  transfers between devices with their start and end apart: 22 -> 22, of which waited for: 13 -> 11; matrix products, arithmetic and copies ran while one was open for 26% -> 21% of each run, Pallas kernels for 0% -> 0%
where the time goes in v4:
time: 228 us; the launch traced here: 227 us
  matrix products  64.8 us (28%)
  waiting for transfers between devices  61.9 us (27%)
  starting transfers between devices  35.7 us (16%)
  local copies, waits for them, and re-layouts  28.5 us (12%)
  other arithmetic  20.8 us (9%)
  between operations  15.1 us (7%)
    ppermute x9, waiting for transfers between devices, _gather(): lax.ppermute(d, name, perm)  32.5 us
    ppermute x9, waiting for transfers between devices, _scatter_sum(): acc = acc + lax.ppermute(piece, name, perm)  28.7 us
    dot_general x1, matrix products, shards(): jnp.dot(chooser, jnp.concatenate([high.astype(jnp.bfloat16), low], axis=0...  24.9 us
    dot_general x1, matrix products, shards(): jnp.einsum('sqn,snd->sqd', picker, every_x, preferred_element_type=jnp.fl...  17 us
    dot_general x1, matrix products, shards(): jnp.dot(residual_vectors, orthogonal_quantizer_turn, preferred_element_ty...  14.8 us
    ppermute x9, starting transfers between devices, _scatter_sum(): acc = acc + lax.ppermute(piece, name, perm)  14.6 us
    ppermute x9, starting transfers between devices, _gather(): lax.ppermute(d, name, perm)  10.3 us
    all_to_all x1, starting transfers between devices, shards(): lax.all_to_all(tables, 'owners', split_axis=0, concat_axis=0, tiled=True)  7.12 us
  transfers between devices with their start and end apart: 22, of which 11 were waited for; matrix products, arithmetic and copies ran while one was open for 21% of the time, Pallas kernels for 0%

profile of v4, /device:TPU:1, one launch (start us, length us, event | category | flops | bytes accessed | tf_op | source)
XLA Modules:
  0.0 226.9 jit_solution(4158355344023308197)
XLA Ops:
  8.6 2.7 %multiply_reduce_fusion = f32[1024]{0:T(1024)S(1)} fusion(f32[1024,1024]{1,0:T(8,128)} %param.7), kind=kLoop, calls=%fused_computation.28 | loop fusion | flops 2096128 | bytes 4198400 | tf_op jit(solution)/shard_map/reduce_sum | solution.py:88
  12.0 4.0 %fusion.59 = (f32[1024]{0:T(1024)S(1)}, f32[1024,1024]{0,1:T(8,128)S(1)}) fusion(f32[]{:T(128)} %bitcast.111, f32[1024]{0:T(1024)S(1)} %multiply_reduce_fusion, bf16[1024,1024]{1,0:T(8,128)(2,1)} %param.6, f32[1024,1024]{1,0:T(8,128)S(1)} %copy-done.2), kind=kOutput, calls=%fused_computation.96 | convolution fusion | flops 2152725504 | bytes 10493956 | tf_op jit(solution)/shard_map/dot_general | solution.py:89
  18.2 4.2 %fusion.30 = f32[1152,1024]{1,0:T(8,128)} fusion(bf16[1024,1024]{1,0:T(8,128)(2,1)S(1)} %copy-done.6, bf16[1024,1024]{0,1:T(8,128)(2,1)S(1)} %get-tuple-element.11), kind=kOutput, calls=%fused_computation.35 | convolution fusion | flops 2415919104 | bytes 8912896 | tf_op jit(solution)/shard_map/dot_general | solution.py:98
  22.4 1.4 dynamic_update_slice.49
  23.9 3.8 %dynamic-slice_bitcast_fusion = f32[576,1024]{1,0:T(8,128)} fusion(f32[2,576,1024]{2,1,0:T(8,128)} %bitcast.120, s32[]{:T(128)S(6)} %select_n.196), kind=kLoop, calls=%fused_computation.34 | loop fusion | bytes 4718596 | tf_op jit(solution)/shard_map/jit(dynamic_index_in_dim)/squeeze | solution.py:36
  27.7 1.2 collective-permute-start
  28.9 4.5 %gather_fusion = s32[1024]{0:T(1024)S(1)} fusion(s32[1024]{0:T(1024)S(1)} %copy-done.1, s32[1024]{0:T(1024)S(1)} %broadcast_clamp_fusion), kind=kCustom, calls=%fused_computation | custom fusion | bytes 12288 | tf_op jit(solution)/shard_map/jit(_take)/gather | solution.py:109
  33.4 3.1 %bitcast_add_fusion = f32[576,1024]{1,0:T(8,128)S(1)} fusion(f32[576,1024]{1,0:T(8,128)} %collective-permute-done, f32[2,576,1024]{2,1,0:T(8,128)} %bitcast.121, s32[]{:T(128)S(6)} %select_n.195), kind=kLoop, calls=%fused_computation.33 | loop fusion | flops 589824 | bytes 7077892 | tf_op jit(solution)/shard_map/add | solution.py:37
  36.5 1.4 copy-done.5
  37.9 1.2 dynamic-slice_bitcast_fusion.3
  39.1 1.4 collective-permute-start.1
  40.5 1.4 collective-permute-start.3
  41.9 1.6 collective-permute-start.2
  43.5 2.3 reduce-window.6
  46.3 9.3 %collective-permute-done.1 = f32[144,1024]{1,0:T(8,128)S(1)} collective-permute-done((f32[144,1024]{1,0:T(8,128)}, f32[144,1024]{1,0:T(8,128)S(1)}, u32[]{:S(2)}, u32[]{:S(2)}) %collective-permute-start.1) | collective-permute-done | bytes 589856 | tf_op jit(solution)/shard_map/ppermute | solution.py:44
  56.5 12.7 %collective-permute-done.2 = f32[144,1024]{1,0:T(8,128)} collective-permute-done((f32[144,1024]{1,0:T(8,128)S(1)}, f32[144,1024]{1,0:T(8,128)}, u32[]{:S(2)}, u32[]{:S(2)}) %collective-permute-start.2) | collective-permute-done | bytes 589856 | tf_op jit(solution)/shard_map/ppermute | solution.py:44
  69.2 1.8 fusion.36
  71.1 1.7 collective-permute-start.4
  72.8 2.7 %collective-permute-start.6 = (f32[36,1024]{1,0:T(8,128)S(1)}, f32[36,1024]{1,0:T(8,128)S(1)}, u32[]{:S(2)}, u32[]{:S(2)}) collective-permute-start(f32[36,1024]{1,0:T(8,128)S(1)} %get-tuple-element.16), channel_id=1, source_target_pairs={{0,96},{8,104},{16,112},{24,120},{32,0},{40,8},{48,16},{56,24},{64... | collective-permute-start | bytes 442376 | tf_op jit(solution)/shard_map/ppermute | solution.py:44
  75.5 1.1 collective-permute-start.5
  76.6 2.2 collective-permute-done.4
  78.9 4.4 %collective-permute-done.5 = f32[36,1024]{1,0:T(8,128)S(1)} collective-permute-done((f32[36,1024]{1,0:T(8,128)S(1)}, f32[36,1024]{1,0:T(8,128)S(1)}, u32[]{:S(2)}, u32[]{:S(2)}) %collective-permute-start.5) | collective-permute-done | bytes 147488 | tf_op jit(solution)/shard_map/ppermute | solution.py:44
  83.3 1.7 collective-permute-start.7
  85.1 1.3 collective-permute-start.9
  86.3 1.7 collective-permute-start.8
  88.0 4.5 %scatter_custom_fusion.1 = s32[4096]{0:T(1024)S(1)} fusion(s32[1024]{0:T(1024)S(1)} %bitcast.132, s32[1024]{0:T(1024)S(1)} %copy-done.8, s32[]{:T(128)} %constant.233.clone.1), kind=kCustom, calls=%fused_computation.81 | custom fusion | bytes 16388 | tf_op jit(solution)/shard_map/scatter | solution.py:117
  92.5 4.3 %scatter_custom_fusion = s32[4096]{0:T(1024)S(1)} fusion(s32[1024]{0:T(1024)S(1)} %bitcast.133, s32[1024]{0:T(1024)S(1)} %iota.19, s32[]{:T(128)} %constant.230.clone.1), kind=kCustom, calls=%fused_computation.84 | custom fusion | bytes 16388 | tf_op jit(solution)/shard_map/scatter | solution.py:115
  98.0 7.1 %all-to-all-start = ((s32[8,2,512]{2,1,0:T(2,128)}), s32[8,2,512]{2,1,0:T(2,128)S(1)}, u32[]{:S(2)}, u32[]{:S(2)}) async-start(s32[8,2,512]{2,1,0:T(2,128)} %pad_add_fusion), calls=%async_computation | async-start | bytes 65536 | tf_op jit(solution)/shard_map/all_to_all | solution.py:119
  105.1 2.9 %collective-permute-start.11 = (f32[9,1024]{1,0:T(8,128)S(1)}, f32[9,1024]{1,0:T(8,128)S(1)}, u32[]{:S(2)}, u32[]{:S(2)}) collective-permute-start(f32[9,1024]{1,0:T(8,128)S(1)} %get-tuple-element.9), channel_id=1, source_target_pairs={{0,4},{1,5},{2,6},{3,7},{4,0},{5,1},{6,2},{7,3},{8,12},{9,13},{10,... | collective-permute-start | bytes 110600 | tf_op jit(solution)/shard_map/ppermute | solution.py:60
  108.8 1.7 collective-permute-done.11
  111.5 0.9 collective-permute-start.13
  112.5 1.9 collective-permute-start.15
  114.6 2.3 %collective-permute-done.13 = f32[36,1024]{1,0:T(8,128)S(1)} collective-permute-done((f32[36,1024]{1,0:T(8,128)S(1)}, f32[36,1024]{1,0:T(8,128)S(1)}, u32[]{:S(2)}, u32[]{:S(2)}) %collective-permute-start.13) | collective-permute-done | bytes 147488 | tf_op jit(solution)/shard_map/ppermute | solution.py:60
  116.9 3.7 %collective-permute-done.14 = f32[36,1024]{1,0:T(8,128)S(1)} collective-permute-done((f32[36,1024]{1,0:T(8,128)S(1)}, f32[36,1024]{1,0:T(8,128)S(1)}, u32[]{:S(2)}, u32[]{:S(2)}) %collective-permute-start.14) | collective-permute-done | bytes 147488 | tf_op jit(solution)/shard_map/ppermute | solution.py:60
  120.8 17.0 %fusion.14 = bf16[8,512,1024]{2,1,0:T(8,128)(2,1)} fusion(bf16[8,1024,1024]{2,1,0:T(8,128)(2,1)} %bitcast.134, s32[8,512]{1,0:T(8,128)S(1)} %bitcast.129), kind=kOutput, calls=%fused_computation.16 | convolution fusion | flops 8598323200 | bytes 25182208 | tf_op jit(solution)/shard_map/sqn,snd->sqd/dot_general | solution.py:124
  138.4 1.7 collective-permute-start.17
  140.1 0.9 collective-permute-start.18
  141.3 10.5 %collective-permute-done.16 = f32[144,1024]{1,0:T(8,128)} collective-permute-done((f32[144,1024]{1,0:T(8,128)S(1)}, f32[144,1024]{1,0:T(8,128)}, u32[]{:S(2)}, u32[]{:S(2)}) %collective-permute-start.16) | collective-permute-done | bytes 589856 | tf_op jit(solution)/shard_map/ppermute | solution.py:60
  151.8 1.1 bitcast_dynamic-update-slice_fusion.4
  152.9 10.8 %collective-permute-done.17 = f32[144,1024]{1,0:T(8,128)S(1)} collective-permute-done((f32[144,1024]{1,0:T(8,128)S(1)}, f32[144,1024]{1,0:T(8,128)S(1)}, u32[]{:S(2)}, u32[]{:S(2)}) %collective-permute-start.17) | collective-permute-done | bytes 589856 | tf_op jit(solution)/shard_map/ppermute | solution.py:60
  163.8 2.7 %collective-permute-done.18 = f32[144,1024]{1,0:T(8,128)S(1)} collective-permute-done((f32[144,1024]{1,0:T(8,128)S(1)}, f32[144,1024]{1,0:T(8,128)S(1)}, u32[]{:S(2)}, u32[]{:S(2)}) %collective-permute-start.18) | collective-permute-done | bytes 589856 | tf_op jit(solution)/shard_map/ppermute | solution.py:60
  166.5 2.5 %collective-permute-start.19 = (f32[576,1024]{1,0:T(8,128)S(1)}, f32[576,1024]{1,0:T(8,128)S(1)}, u32[]{:S(2)}, u32[]{:S(2)}) collective-permute-start(f32[576,1024]{1,0:T(8,128)S(1)} %bitcast.118), channel_id=1, source_target_pairs={{0,1},{1,0},{2,3},{3,2},{4,5},{5,4},{6,7},{7,6},{8,9},{9,8},{10,11... | collective-permute-start | bytes 7077896 | tf_op jit(solution)/shard_map/ppermute | solution.py:53
  169.1 4.0 %iota_compare_fusion = pred[4096,1024]{1,0:T(32,128)(4,1)} fusion(s32[4096]{0:T(1024)S(1)} %bitcast.123), kind=kLoop, calls=%fused_computation.8 | loop fusion | flops 4194304 | bytes 4210688 | tf_op jit(solution)/shard_map/eq | solution.py:133
  174.3 1.6 copy-done.3
  175.9 1.9 reduce-precision_convert_fusion
  177.7 2.7 %fusion.19 = bf16[1024,1024]{1,0:T(8,128)(2,1)} fusion(f32[1024,1024]{1,0:T(8,128)S(1)} %get-tuple-element.7), kind=kLoop, calls=%fused_computation.19 | loop fusion | flops 3145728 | bytes 6291456 | tf_op jit(solution)/shard_map/convert_element_type | solution.py:144
  180.4 24.9 %fusion.73 = bf16[4096,1024]{1,0:T(8,128)(2,1)} fusion(pred[4096]{0:T(1024)(128)(4,1)S(1)} %broadcast_compare_fusion, pred[4096,1024]{1,0:T(32,128)(4,1)} %iota_compare_fusion, bf16[4096,1024]{1,0:T(8,128)(2,1)} %bitcast.135, bf16[1024,1024]{1,0:T(8,128)(2,1)} %fusion.19, bf16[1024,1024]{1,0:T(8,128)(2,1)} %get-tuple-element.6), kind=kOutput, calls=%fused_computation.12.clone.clone.clone.1 | convolution fusion | flops 17213423616 | bytes 25169920 | tf_op jit(solution)/shard_map/dot_general | solution.py:145
  205.3 14.8 %fusion.11 = bf16[4096,1024]{1,0:T(8,128)(2,1)} fusion(bf16[1024,1024]{1,0:T(8,128)(2,1)S(1)} %copy-done, bf16[4096,1024]{1,0:T(8,128)(2,1)} %fusion.73), kind=kOutput, calls=%fused_computation.15 | convolution fusion | flops 8594128896 | bytes 18874368 | tf_op jit(solution)/shard_map/dot_general | solution.py:152
  (75 shorter events, 10.7 us)
Async XLA Ops:
  7.2 198.1 %copy-start = (bf16[1024,1024]{1,0:T(8,128)(2,1)S(1)}, bf16[1024,1024]{1,0:T(8,128)(2,1)}, u32[]{:S(2)}) copy-start(bf16[1024,1024]{1,0:T(8,128)(2,1)} %param.11) | copy-start | bytes 6291460
  7.2 113.6 %all-gather.3.cloned.1.call-start = ((), (), s32[]{:S(2)}) async-start(), calls=%async_computation.1 | async-start | bytes 18874368 | tf_op jit(solution)/shard_map/all_gather | solution.py:108
  8.6 3.5 %copy-start.2 = (f32[1024,1024]{1,0:T(8,128)S(1)}, f32[1024,1024]{1,0:T(8,128)}, u32[]{:S(2)}) copy-start(f32[1024,1024]{1,0:T(8,128)} %param.7) | copy-start | bytes 12582916
  16.7 1.6 copy-start.6
  22.4 6.4 %copy-start.8 = (s32[1024]{0:T(1024)S(1)}, s32[1024]{0:T(1024)}, u32[]{:S(2)}) copy-start(s32[1024]{0:T(1024)} %param.9) | copy-start | bytes 12292
  22.4 6.4 %copy-start.1 = (s32[1024]{0:T(1024)S(1)}, s32[1024]{0:T(1024)}, u32[]{:S(2)}) copy-start(s32[1024]{0:T(1024)} %param.10) | copy-start | bytes 12292
  27.7 5.7 %collective-permute-start = (f32[576,1024]{1,0:T(8,128)}, f32[576,1024]{1,0:T(8,128)}, u32[]{:S(2)}, u32[]{:S(2)}) collective-permute-start(f32[576,1024]{1,0:T(8,128)} %dynamic-slice_bitcast_fusion), channel_id=1, source_target_pairs={{0,1},{1,0},{2,3},{3,2},{4,5},{5,4},{6,7},{7,6},{8,9},{9,8},{10,11... | collective-permute-start | bytes 7077896 | tf_op jit(solution)/shard_map/ppermute | solution.py:37
  36.5 1.4 copy-start.5
  39.1 16.6 %collective-permute-start.1 = (f32[144,1024]{1,0:T(8,128)}, f32[144,1024]{1,0:T(8,128)S(1)}, u32[]{:S(2)}, u32[]{:S(2)}) collective-permute-start(f32[144,1024]{1,0:T(8,128)} %get-tuple-element.12), channel_id=1, source_target_pairs={{0,8},{8,16},{16,24},{24,0},{32,40},{40,48},{48,56},{56,32},{64,72... | collective-permute-start | bytes 1769480 | tf_op jit(solution)/shard_map/ppermute | solution.py:44
  40.5 15.2 %collective-permute-start.3 = (f32[144,1024]{1,0:T(8,128)}, f32[144,1024]{1,0:T(8,128)}, u32[]{:S(2)}, u32[]{:S(2)}) collective-permute-start(f32[144,1024]{1,0:T(8,128)} %get-tuple-element.13), channel_id=1, source_target_pairs={{0,24},{8,0},{16,8},{24,16},{32,56},{40,32},{48,40},{56,48},{64,88... | collective-permute-start | bytes 1769480 | tf_op jit(solution)/shard_map/ppermute | solution.py:44
  41.9 27.3 %collective-permute-start.2 = (f32[144,1024]{1,0:T(8,128)S(1)}, f32[144,1024]{1,0:T(8,128)}, u32[]{:S(2)}, u32[]{:S(2)}) collective-permute-start(f32[144,1024]{1,0:T(8,128)S(1)} %get-tuple-element.14), channel_id=1, source_target_pairs={{0,16},{8,24},{16,0},{24,8},{32,48},{40,56},{48,32},{56,40},{64,80... | collective-permute-start | bytes 1769480 | tf_op jit(solution)/shard_map/ppermute | solution.py:44
  55.7 0.8 copy-start.7
  71.1 7.7 %collective-permute-start.4 = (f32[36,1024]{1,0:T(8,128)S(1)}, f32[36,1024]{1,0:T(8,128)S(1)}, u32[]{:S(2)}, u32[]{:S(2)}) collective-permute-start(f32[36,1024]{1,0:T(8,128)S(1)} %get-tuple-element.15), channel_id=1, source_target_pairs={{0,32},{8,40},{16,48},{24,56},{32,64},{40,72},{48,80},{56,88},{64,... | collective-permute-start | bytes 442376 | tf_op jit(solution)/shard_map/ppermute | solution.py:44
  72.8 6.1 %collective-permute-start.6 = (f32[36,1024]{1,0:T(8,128)S(1)}, f32[36,1024]{1,0:T(8,128)S(1)}, u32[]{:S(2)}, u32[]{:S(2)}) collective-permute-start(f32[36,1024]{1,0:T(8,128)S(1)} %get-tuple-element.16), channel_id=1, source_target_pairs={{0,96},{8,104},{16,112},{24,120},{32,0},{40,8},{48,16},{56,24},{64... | collective-permute-start | bytes 442376 | tf_op jit(solution)/shard_map/ppermute | solution.py:44
  75.5 7.7 %collective-permute-start.5 = (f32[36,1024]{1,0:T(8,128)S(1)}, f32[36,1024]{1,0:T(8,128)S(1)}, u32[]{:S(2)}, u32[]{:S(2)}) collective-permute-start(f32[36,1024]{1,0:T(8,128)S(1)} %get-tuple-element.17), channel_id=1, source_target_pairs={{0,64},{8,72},{16,80},{24,88},{32,96},{40,104},{48,112},{56,120},{... | collective-permute-start | bytes 442376 | tf_op jit(solution)/shard_map/ppermute | solution.py:44
  83.3 13.5 %collective-permute-start.7 = (f32[9,1024]{1,0:T(8,128)S(1)}, f32[9,1024]{1,0:T(8,128)S(1)}, u32[]{:S(2)}, u32[]{:S(2)}) collective-permute-start(f32[9,1024]{1,0:T(8,128)S(1)} %get-tuple-element.18), channel_id=1, source_target_pairs={{0,2},{1,3},{2,4},{3,5},{4,6},{5,7},{6,0},{7,1},{8,10},{9,11},{10,... | collective-permute-start | bytes 110600 | tf_op jit(solution)/shard_map/ppermute | solution.py:44
  85.1 11.8 %collective-permute-start.9 = (f32[9,1024]{1,0:T(8,128)S(1)}, f32[9,1024]{1,0:T(8,128)S(1)}, u32[]{:S(2)}, u32[]{:S(2)}) collective-permute-start(f32[9,1024]{1,0:T(8,128)S(1)} %get-tuple-element.19), channel_id=1, source_target_pairs={{0,6},{1,7},{2,0},{3,1},{4,2},{5,3},{6,4},{7,5},{8,14},{9,15},{10,... | collective-permute-start | bytes 110600 | tf_op jit(solution)/shard_map/ppermute | solution.py:44
  86.3 10.6 %collective-permute-start.8 = (f32[9,1024]{1,0:T(8,128)S(1)}, f32[9,1024]{1,0:T(8,128)S(1)}, u32[]{:S(2)}, u32[]{:S(2)}) collective-permute-start(f32[9,1024]{1,0:T(8,128)S(1)} %get-tuple-element.20), channel_id=1, source_target_pairs={{0,4},{1,5},{2,6},{3,7},{4,0},{5,1},{6,2},{7,3},{8,12},{9,13},{10,... | collective-permute-start | bytes 110600 | tf_op jit(solution)/shard_map/ppermute | solution.py:44
  97.0 11.9 %collective-permute-start.10 = (f32[9,1024]{1,0:T(8,128)S(1)}, f32[9,1024]{1,0:T(8,128)S(1)}, u32[]{:S(2)}, u32[]{:S(2)}) collective-permute-start(f32[9,1024]{1,0:T(8,128)S(1)} %get-tuple-element.9), channel_id=1, source_target_pairs={{0,2},{1,3},{2,4},{3,5},{4,6},{5,7},{6,0},{7,1},{8,10},{9,11},{10,... | collective-permute-start | bytes 110600 | tf_op jit(solution)/shard_map/ppermute | solution.py:60
  98.0 14.4 %all-to-all-start = ((s32[8,2,512]{2,1,0:T(2,128)}), s32[8,2,512]{2,1,0:T(2,128)S(1)}, u32[]{:S(2)}, u32[]{:S(2)}) async-start(s32[8,2,512]{2,1,0:T(2,128)} %pad_add_fusion), calls=%async_computation | async-start | bytes 65536 | tf_op jit(solution)/shard_map/all_to_all | solution.py:119
  105.1 5.5 %collective-permute-start.11 = (f32[9,1024]{1,0:T(8,128)S(1)}, f32[9,1024]{1,0:T(8,128)S(1)}, u32[]{:S(2)}, u32[]{:S(2)}) collective-permute-start(f32[9,1024]{1,0:T(8,128)S(1)} %get-tuple-element.9), channel_id=1, source_target_pairs={{0,4},{1,5},{2,6},{3,7},{4,0},{5,1},{6,2},{7,3},{8,12},{9,13},{10,... | collective-permute-start | bytes 110600 | tf_op jit(solution)/shard_map/ppermute | solution.py:60
  107.9 3.5 %collective-permute-start.12 = (f32[9,1024]{1,0:T(8,128)S(1)}, f32[9,1024]{1,0:T(8,128)S(1)}, u32[]{:S(2)}, u32[]{:S(2)}) collective-permute-start(f32[9,1024]{1,0:T(8,128)S(1)} %get-tuple-element.9), channel_id=1, source_target_pairs={{0,6},{1,7},{2,0},{3,1},{4,2},{5,3},{6,4},{7,5},{8,14},{9,15},{10,... | collective-permute-start | bytes 110600 | tf_op jit(solution)/shard_map/ppermute | solution.py:60
  111.5 5.4 %collective-permute-start.13 = (f32[36,1024]{1,0:T(8,128)S(1)}, f32[36,1024]{1,0:T(8,128)S(1)}, u32[]{:S(2)}, u32[]{:S(2)}) collective-permute-start(f32[36,1024]{1,0:T(8,128)S(1)} %reshape.104), channel_id=1, source_target_pairs={{0,32},{8,40},{16,48},{24,56},{32,64},{40,72},{48,80},{56,88},{64,... | collective-permute-start | bytes 442376 | tf_op jit(solution)/shard_map/ppermute | solution.py:60
  112.5 8.2 %collective-permute-start.15 = (f32[36,1024]{1,0:T(8,128)S(1)}, f32[36,1024]{1,0:T(8,128)S(1)}, u32[]{:S(2)}, u32[]{:S(2)}) collective-permute-start(f32[36,1024]{1,0:T(8,128)S(1)} %reshape.104), channel_id=1, source_target_pairs={{0,96},{8,104},{16,112},{24,120},{32,0},{40,8},{48,16},{56,24},{64... | collective-permute-start | bytes 442376 | tf_op jit(solution)/shard_map/ppermute | solution.py:60
  114.4 6.3 %collective-permute-start.14 = (f32[36,1024]{1,0:T(8,128)S(1)}, f32[36,1024]{1,0:T(8,128)S(1)}, u32[]{:S(2)}, u32[]{:S(2)}) collective-permute-start(f32[36,1024]{1,0:T(8,128)S(1)} %reshape.104), channel_id=1, source_target_pairs={{0,64},{8,72},{16,80},{24,88},{32,96},{40,104},{48,112},{56,120},{... | collective-permute-start | bytes 442376 | tf_op jit(solution)/shard_map/ppermute | solution.py:60
  137.8 14.0 %collective-permute-start.16 = (f32[144,1024]{1,0:T(8,128)S(1)}, f32[144,1024]{1,0:T(8,128)}, u32[]{:S(2)}, u32[]{:S(2)}) collective-permute-start(f32[144,1024]{1,0:T(8,128)S(1)} %reshape.105), channel_id=1, source_target_pairs={{0,8},{8,16},{16,24},{24,0},{32,40},{40,48},{48,56},{56,32},{64,72... | collective-permute-start | bytes 1769480 | tf_op jit(solution)/shard_map/ppermute | solution.py:60
  138.4 25.3 %collective-permute-start.17 = (f32[144,1024]{1,0:T(8,128)S(1)}, f32[144,1024]{1,0:T(8,128)S(1)}, u32[]{:S(2)}, u32[]{:S(2)}) collective-permute-start(f32[144,1024]{1,0:T(8,128)S(1)} %reshape.105), channel_id=1, source_target_pairs={{0,16},{8,24},{16,0},{24,8},{32,48},{40,56},{48,32},{56,40},{64,80... | collective-permute-start | bytes 1769480 | tf_op jit(solution)/shard_map/ppermute | solution.py:60
  140.1 26.4 %collective-permute-start.18 = (f32[144,1024]{1,0:T(8,128)S(1)}, f32[144,1024]{1,0:T(8,128)S(1)}, u32[]{:S(2)}, u32[]{:S(2)}) collective-permute-start(f32[144,1024]{1,0:T(8,128)S(1)} %reshape.105), channel_id=1, source_target_pairs={{0,24},{8,0},{16,8},{24,16},{32,56},{40,32},{48,40},{56,48},{64,88... | collective-permute-start | bytes 1769480 | tf_op jit(solution)/shard_map/ppermute | solution.py:60
  166.5 7.5 %collective-permute-start.19 = (f32[576,1024]{1,0:T(8,128)S(1)}, f32[576,1024]{1,0:T(8,128)S(1)}, u32[]{:S(2)}, u32[]{:S(2)}) collective-permute-start(f32[576,1024]{1,0:T(8,128)S(1)} %bitcast.118), channel_id=1, source_target_pairs={{0,1},{1,0},{2,3},{3,2},{4,5},{5,4},{6,7},{7,6},{8,9},{9,8},{10,11... | collective-permute-start | bytes 7077896 | tf_op jit(solution)/shard_map/ppermute | solution.py:53
  173.7 2.2 copy-start.3
  177.7 27.5 %copy-start.4 = (f32[1024,1024]{1,0:T(8,128)}, f32[1024,1024]{1,0:T(8,128)S(1)}, u32[]{:S(2)}) copy-start(f32[1024,1024]{1,0:T(8,128)S(1)} %get-tuple-element.7) | copy-start | bytes 12582916
Sparse Core Ops, SparseCore 0:
  9.7 91.2 all-gather.2

commit v5 on v4

--- a/solution.py
+++ b/solution.py
@@ -124,16 +124,16 @@
     recv_x = jnp.einsum(
         "sqn,snd->sqd", picker, every_x, preferred_element_type=jnp.float32
     ).astype(jnp.bfloat16).reshape(groups * CAP, width)
-    partial, recv_x = lax.optimization_barrier((partial, recv_x))
-    for axis in ("y", "core"):
-        partial = _gather(partial, axis)
-    total = partial
 
     valid = recv_label >= 0
     chooser = (recv_label[:, None] == jnp.arange(clusters, dtype=jnp.int32)[None, :]).astype(
         jnp.bfloat16
     )
     chooser = jnp.concatenate([chooser, chooser], axis=1)
+    partial = _gather(partial, "y")
+    partial, recv_x, chooser = lax.optimization_barrier((partial, recv_x, chooser))
+    partial = _gather(partial, "core")
+    total = partial
 
     total_sums = total[:clusters]
     total_counts = total[clusters]

time: 228 us -> 227 us (level)
  waiting for transfers between devices: 61.9 us -> 50.7 us
  other arithmetic: 20.8 us -> 30.6 us
  local copies, waits for them, and re-layouts: 28.5 us -> 38 us
  matrix products: 64.8 us -> 58.7 us
  starting transfers between devices: 35.7 us -> 33 us
    dot_general x1 -> x0, matrix products: 24.9 us -> none  [shards(): jnp.dot(chooser, jnp.concatenate([high.astype(jnp.bfloat16), low], axis=0...]
    dot_general x1, matrix products: 14.8 us -> 33.7 us  [shards(): jnp.dot(residual_vectors, orthogonal_quantizer_turn, preferred_element_ty...]
    ppermute x9, waiting for transfers between devices: 32.5 us -> 20.8 us  [_gather(): lax.ppermute(d, name, perm)]
    concatenate x0 -> x1, other arithmetic: none -> 9.76 us  [shards(): chooser = jnp.concatenate([chooser, chooser], axis=1)]
    ppermute x9, waiting for transfers between devices: 28.7 us -> 24.4 us  [_scatter_sum(): acc = acc + lax.ppermute(piece, name, perm)]
    dynamic_update_slice x9, local copies, waits for them, and re-layouts: 1.28 us -> 4.8 us  [_gather(): lax.dynamic_update_index_in_dim(out, lax.ppermute(d, name, perm), (me - s...]
    all_to_all x1, waiting for transfers between devices: 0.01 us -> 3.23 us  [shards(): lax.all_to_all(tables, 'owners', split_axis=0, concat_axis=0, tiled=True)]
    dynamic_update_slice x3, local copies, waits for them, and re-layouts: 0.36 us -> 3.05 us  [_gather(): out = lax.dynamic_update_index_in_dim(out, d, me, 0)]
  transfers between devices with their start and end apart: 22 -> 22, of which waited for: 11 -> 7; matrix products, arithmetic and copies ran while one was open for 21% -> 30% of each run, Pallas kernels for 0% -> 0%
where the time goes in v5:
time: 227 us; the launch traced here: 226 us
  matrix products  58.7 us (26%)
  waiting for transfers between devices  50.7 us (22%)
  local copies, waits for them, and re-layouts  38 us (17%)
  starting transfers between devices  33 us (15%)
  other arithmetic  30.6 us (13%)
  between operations  15.2 us (7%)
    dot_general x1, matrix products, shards(): jnp.dot(residual_vectors, orthogonal_quantizer_turn, preferred_element_ty...  33.7 us
    ppermute x9, waiting for transfers between devices, _scatter_sum(): acc = acc + lax.ppermute(piece, name, perm)  24.4 us
    ppermute x9, waiting for transfers between devices, _gather(): lax.ppermute(d, name, perm)  20.8 us
    dot_general x1, matrix products, shards(): jnp.einsum('sqn,snd->sqd', picker, every_x, preferred_element_type=jnp.fl...  16.9 us
    ppermute x9, starting transfers between devices, _scatter_sum(): acc = acc + lax.ppermute(piece, name, perm)  14.6 us
    ppermute x9, starting transfers between devices, _gather(): lax.ppermute(d, name, perm)  11 us
    concatenate x1, other arithmetic, shards(): chooser = jnp.concatenate([chooser, chooser], axis=1)  9.76 us
    unnamed x19, local copies, waits for them, and re-layouts  5.77 us
  transfers between devices with their start and end apart: 22, of which 7 were waited for; matrix products, arithmetic and copies ran while one was open for 30% of the time, Pallas kernels for 0%

profile of v5, /device:TPU:1, one launch (start us, length us, event | category | flops | bytes accessed | tf_op | source)
XLA Modules:
  0.0 226.1 jit_solution(17997525416207469255)
XLA Ops:
  8.6 2.7 %multiply_reduce_fusion = f32[1024]{0:T(1024)S(1)} fusion(f32[1024,1024]{1,0:T(8,128)} %param.7), kind=kLoop, calls=%fused_computation.25 | loop fusion | flops 2096128 | bytes 4198400 | tf_op jit(solution)/shard_map/reduce_sum | solution.py:88
  12.0 4.0 %fusion.43 = (f32[1024]{0:T(1024)S(1)}, f32[1024,1024]{0,1:T(8,128)S(1)}) fusion(f32[]{:T(128)} %bitcast.111, f32[1024]{0:T(1024)S(1)} %multiply_reduce_fusion, bf16[1024,1024]{1,0:T(8,128)(2,1)} %param.6, f32[1024,1024]{1,0:T(8,128)S(1)} %copy-done.2), kind=kOutput, calls=%fused_computation.92 | convolution fusion | flops 2152725504 | bytes 10493956 | tf_op jit(solution)/shard_map/dot_general | solution.py:89
  18.2 4.2 %fusion.17 = f32[1152,1024]{1,0:T(8,128)} fusion(bf16[1024,1024]{1,0:T(8,128)(2,1)S(1)} %copy-done.6, bf16[1024,1024]{0,1:T(8,128)(2,1)S(1)} %get-tuple-element.13), kind=kOutput, calls=%fused_computation.32 | convolution fusion | flops 2415919104 | bytes 8912896 | tf_op jit(solution)/shard_map/dot_general | solution.py:98
  22.4 1.4 dynamic_update_slice.49
  23.9 3.8 %dynamic-slice_bitcast_fusion = f32[576,1024]{1,0:T(8,128)} fusion(f32[2,576,1024]{2,1,0:T(8,128)} %bitcast.118, s32[]{:T(128)S(6)} %select_n.196), kind=kLoop, calls=%fused_computation.31 | loop fusion | bytes 4718596 | tf_op jit(solution)/shard_map/jit(dynamic_index_in_dim)/squeeze | solution.py:36
  27.7 1.2 collective-permute-start
  28.9 4.5 %gather_fusion = s32[1024]{0:T(1024)S(1)} fusion(s32[1024]{0:T(1024)S(1)} %copy-done.1, s32[1024]{0:T(1024)S(1)} %broadcast_clamp_fusion), kind=kCustom, calls=%fused_computation | custom fusion | bytes 12288 | tf_op jit(solution)/shard_map/jit(_take)/gather | solution.py:109
  33.4 2.3 %reduce-window.6 = s32[8,8,128]{2,1,0:T(8,128)S(1)} reduce-window(s32[8,8,128]{2,1,0:T(8,128)S(1)} %fusion.31, s32[]{:T(128)} %constant.230.clone.1), window={size=1x1x128 pad=0_0x0_0x127_0}, to_apply=%region_0.0 | reduce-window | flops 1040384 | bytes 65540 | tf_op jit(solution)/shard_map/reduce-window
  35.7 2.9 %bitcast_add_fusion = f32[576,1024]{1,0:T(8,128)S(1)} fusion(f32[576,1024]{1,0:T(8,128)} %collective-permute-done, f32[2,576,1024]{2,1,0:T(8,128)} %bitcast.119, s32[]{:T(128)S(6)} %select_n.195), kind=kLoop, calls=%fused_computation.30 | loop fusion | flops 589824 | bytes 7077892 | tf_op jit(solution)/shard_map/add | solution.py:37
  38.6 1.4 copy-done.5
  40.0 1.2 dynamic-slice_bitcast_fusion.3
  41.2 1.4 collective-permute-start.1
  42.6 1.4 collective-permute-start.3
  44.0 1.6 collective-permute-start.2
  46.3 11.5 %collective-permute-done.1 = f32[144,1024]{1,0:T(8,128)S(1)} collective-permute-done((f32[144,1024]{1,0:T(8,128)}, f32[144,1024]{1,0:T(8,128)S(1)}, u32[]{:S(2)}, u32[]{:S(2)}) %collective-permute-start.1) | collective-permute-done | bytes 589856 | tf_op jit(solution)/shard_map/ppermute | solution.py:44
  58.6 12.9 %collective-permute-done.2 = f32[144,1024]{1,0:T(8,128)} collective-permute-done((f32[144,1024]{1,0:T(8,128)S(1)}, f32[144,1024]{1,0:T(8,128)}, u32[]{:S(2)}, u32[]{:S(2)}) %collective-permute-start.2) | collective-permute-done | bytes 589856 | tf_op jit(solution)/shard_map/ppermute | solution.py:44
  71.5 1.8 fusion.23
  74.0 1.8 collective-permute-start.4
  75.8 2.7 %collective-permute-start.6 = (f32[36,1024]{1,0:T(8,128)S(1)}, f32[36,1024]{1,0:T(8,128)S(1)}, u32[]{:S(2)}, u32[]{:S(2)}) collective-permute-start(f32[36,1024]{1,0:T(8,128)S(1)} %get-tuple-element.18), channel_id=1, source_target_pairs={{0,96},{8,104},{16,112},{24,120},{32,0},{40,8},{48,16},{56,24},{64... | collective-permute-start | bytes 442376 | tf_op jit(solution)/shard_map/ppermute | solution.py:44
  78.5 1.2 collective-permute-start.5
  79.7 4.3 %scatter_custom_fusion.1 = s32[4096]{0:T(1024)S(1)} fusion(s32[1024]{0:T(1024)S(1)} %bitcast.130, s32[1024]{0:T(1024)S(1)} %copy-done.8, s32[]{:T(128)} %constant.233.clone.1), kind=kCustom, calls=%fused_computation.77 | custom fusion | bytes 16388 | tf_op jit(solution)/shard_map/scatter | solution.py:117
  84.0 4.3 %scatter_custom_fusion = s32[4096]{0:T(1024)S(1)} fusion(s32[1024]{0:T(1024)S(1)} %bitcast.131, s32[1024]{0:T(1024)S(1)} %iota.19, s32[]{:T(128)} %constant.230.clone.1), kind=kCustom, calls=%fused_computation.80 | custom fusion | bytes 16388 | tf_op jit(solution)/shard_map/scatter | solution.py:115
  88.4 1.0 fusion.25
  89.5 1.5 collective-permute-start.7
  91.0 1.6 collective-permute-start.9
  92.6 1.4 collective-permute-start.8
  94.6 5.7 %all-to-all-start = ((s32[8,2,512]{2,1,0:T(2,128)}), s32[8,2,512]{2,1,0:T(2,128)S(1)}, u32[]{:S(2)}, u32[]{:S(2)}) async-start(s32[8,2,512]{2,1,0:T(2,128)} %pad_add_fusion), calls=%async_computation | async-start | bytes 65536 | tf_op jit(solution)/shard_map/all_to_all | solution.py:119
  100.4 1.4 collective-permute-start.10
  101.8 3.2 %all-to-all-done = s32[8,2,512]{2,1,0:T(2,128)S(1)} async-done(((s32[8,2,512]{2,1,0:T(2,128)}), s32[8,2,512]{2,1,0:T(2,128)S(1)}, u32[]{:S(2)}, u32[]{:S(2)}) %all-to-all-start) | async-done | bytes 32800 | tf_op jit(solution)/shard_map/all_to_all | solution.py:119
  106.0 1.9 collective-permute-start.12
  107.9 1.9 collective-permute-done.11
  110.7 3.9 %iota_compare_fusion = pred[4096,1024]{1,0:T(8,128)(4,1)} fusion(s32[4096]{0:T(1024)S(1)} %bitcast.120), kind=kLoop, calls=%fused_computation.5 | loop fusion | flops 4194304 | bytes 4210688 | tf_op jit(solution)/shard_map/eq | solution.py:129
  114.6 2.0 collective-permute-start.15
  116.9 5.4 %collective-permute-done.14 = f32[36,1024]{1,0:T(8,128)S(1)} collective-permute-done((f32[36,1024]{1,0:T(8,128)S(1)}, f32[36,1024]{1,0:T(8,128)S(1)}, u32[]{:S(2)}, u32[]{:S(2)}) %collective-permute-start.14) | collective-permute-done | bytes 147488 | tf_op jit(solution)/shard_map/ppermute | solution.py:60
  123.2 1.1 collective-permute-start.17
  125.2 9.8 %add_convert_fusion = bf16[4096,2048]{1,0:T(8,128)(2,1)} fusion(pred[4096,1024]{1,0:T(8,128)(4,1)} %iota_compare_fusion), kind=kLoop, calls=%fused_computation.3 | loop fusion | flops 16777216 | bytes 20971520 | tf_op jit(solution)/shard_map/concatenate | solution.py:132
  135.1 1.8 collective-permute-start.18
  136.9 1.7 broadcast_in_dim.90
  139.4 13.5 %collective-permute-done.16 = f32[144,1024]{1,0:T(8,128)} collective-permute-done((f32[144,1024]{1,0:T(8,128)}, f32[144,1024]{1,0:T(8,128)}, u32[]{:S(2)}, u32[]{:S(2)}) %collective-permute-start.16) | collective-permute-done | bytes 589856 | tf_op jit(solution)/shard_map/ppermute | solution.py:60
  152.9 1.9 bitcast_dynamic-update-slice_fusion.4
  154.8 1.9 bitcast_dynamic-update-slice_fusion.3
  157.6 16.9 %fusion.8 = bf16[8,512,1024]{2,1,0:T(8,128)(2,1)} fusion(bf16[8,1024,1024]{2,1,0:T(8,128)(2,1)} %bitcast.132, s32[8,512]{1,0:T(8,128)S(1)} %bitcast.127), kind=kOutput, calls=%fused_computation.13 | convolution fusion | flops 8598323200 | bytes 25182208 | tf_op jit(solution)/shard_map/sqn,snd->sqd/dot_general | solution.py:124
  175.6 2.2 bitcast_dynamic-update-slice_fusion.1
  177.8 1.6 collective-permute-done.19
  179.7 1.9 reduce-precision_convert_fusion
  181.6 2.0 copy-done.4
  183.6 2.0 fusion.9
  185.6 33.7 %fusion.5 = bf16[4096,1024]{1,0:T(8,128)(2,1)} fusion(bf16[1024,1024]{1,0:T(8,128)(2,1)S(1)} %copy-done, pred[4096]{0:T(1024)(128)(4,1)S(1)} %broadcast_compare_fusion, bf16[4096,1024]{1,0:T(8,128)(2,1)} %bitcast.133, bf16[4096,2048]{1,0:T(8,128)(2,1)} %add_convert_fusion, bf16[1024,1024]{1,0:T(8,128)(2,1)} %fusion.9, bf16[1024,1024]{1,0:T(8,128)(2,1)} %get-tuple-element.8), kind=kOutput, calls=%fused_computation.12 | convolution fusion | flops 25799163904 | bytes 39849984 | tf_op jit(solution)/shard_map/dot_general | solution.py:152
  (76 shorter events, 13.7 us)
Async XLA Ops:
  7.2 178.5 %copy-start = (bf16[1024,1024]{1,0:T(8,128)(2,1)S(1)}, bf16[1024,1024]{1,0:T(8,128)(2,1)}, u32[]{:S(2)}) copy-start(bf16[1024,1024]{1,0:T(8,128)(2,1)} %param.11) | copy-start | bytes 6291460
  7.2 150.5 %all-gather.3.cloned.1.call-start = ((), (), s32[]{:S(2)}) async-start(), calls=%async_computation.1 | async-start | bytes 18874368 | tf_op jit(solution)/shard_map/all_gather | solution.py:108
  8.6 3.5 %copy-start.2 = (f32[1024,1024]{1,0:T(8,128)S(1)}, f32[1024,1024]{1,0:T(8,128)}, u32[]{:S(2)}) copy-start(f32[1024,1024]{1,0:T(8,128)} %param.7) | copy-start | bytes 12582916
  16.7 1.6 copy-start.6
  22.4 6.4 %copy-start.8 = (s32[1024]{0:T(1024)S(1)}, s32[1024]{0:T(1024)}, u32[]{:S(2)}) copy-start(s32[1024]{0:T(1024)} %param.9) | copy-start | bytes 12292
  22.4 6.4 %copy-start.1 = (s32[1024]{0:T(1024)S(1)}, s32[1024]{0:T(1024)}, u32[]{:S(2)}) copy-start(s32[1024]{0:T(1024)} %param.10) | copy-start | bytes 12292
  27.7 8.0 %collective-permute-start = (f32[576,1024]{1,0:T(8,128)}, f32[576,1024]{1,0:T(8,128)}, u32[]{:S(2)}, u32[]{:S(2)}) collective-permute-start(f32[576,1024]{1,0:T(8,128)} %dynamic-slice_bitcast_fusion), channel_id=1, source_target_pairs={{0,1},{1,0},{2,3},{3,2},{4,5},{5,4},{6,7},{7,6},{8,9},{9,8},{10,11... | collective-permute-start | bytes 7077896 | tf_op jit(solution)/shard_map/ppermute | solution.py:37
  38.6 1.4 copy-start.5
  41.2 16.6 %collective-permute-start.1 = (f32[144,1024]{1,0:T(8,128)}, f32[144,1024]{1,0:T(8,128)S(1)}, u32[]{:S(2)}, u32[]{:S(2)}) collective-permute-start(f32[144,1024]{1,0:T(8,128)} %get-tuple-element.14), channel_id=1, source_target_pairs={{0,8},{8,16},{16,24},{24,0},{32,40},{40,48},{48,56},{56,32},{64,72... | collective-permute-start | bytes 1769480 | tf_op jit(solution)/shard_map/ppermute | solution.py:44
  42.6 15.2 %collective-permute-start.3 = (f32[144,1024]{1,0:T(8,128)}, f32[144,1024]{1,0:T(8,128)}, u32[]{:S(2)}, u32[]{:S(2)}) collective-permute-start(f32[144,1024]{1,0:T(8,128)} %get-tuple-element.15), channel_id=1, source_target_pairs={{0,24},{8,0},{16,8},{24,16},{32,56},{40,32},{48,40},{56,48},{64,88... | collective-permute-start | bytes 1769480 | tf_op jit(solution)/shard_map/ppermute | solution.py:44
  44.0 27.5 %collective-permute-start.2 = (f32[144,1024]{1,0:T(8,128)S(1)}, f32[144,1024]{1,0:T(8,128)}, u32[]{:S(2)}, u32[]{:S(2)}) collective-permute-start(f32[144,1024]{1,0:T(8,128)S(1)} %get-tuple-element.16), channel_id=1, source_target_pairs={{0,16},{8,24},{16,0},{24,8},{32,48},{40,56},{48,32},{56,40},{64,80... | collective-permute-start | bytes 1769480 | tf_op jit(solution)/shard_map/ppermute | solution.py:44
  57.8 0.8 copy-start.7
  74.0 14.4 %collective-permute-start.4 = (f32[36,1024]{1,0:T(8,128)}, f32[36,1024]{1,0:T(8,128)S(1)}, u32[]{:S(2)}, u32[]{:S(2)}) collective-permute-start(f32[36,1024]{1,0:T(8,128)} %get-tuple-element.17), channel_id=1, source_target_pairs={{0,32},{8,40},{16,48},{24,56},{32,64},{40,72},{48,80},{56,88},{64,... | collective-permute-start | bytes 442376 | tf_op jit(solution)/shard_map/ppermute | solution.py:44
  75.8 12.6 %collective-permute-start.6 = (f32[36,1024]{1,0:T(8,128)S(1)}, f32[36,1024]{1,0:T(8,128)S(1)}, u32[]{:S(2)}, u32[]{:S(2)}) collective-permute-start(f32[36,1024]{1,0:T(8,128)S(1)} %get-tuple-element.18), channel_id=1, source_target_pairs={{0,96},{8,104},{16,112},{24,120},{32,0},{40,8},{48,16},{56,24},{64... | collective-permute-start | bytes 442376 | tf_op jit(solution)/shard_map/ppermute | solution.py:44
  78.5 9.9 %collective-permute-start.5 = (f32[36,1024]{1,0:T(8,128)S(1)}, f32[36,1024]{1,0:T(8,128)}, u32[]{:S(2)}, u32[]{:S(2)}) collective-permute-start(f32[36,1024]{1,0:T(8,128)S(1)} %get-tuple-element.19), channel_id=1, source_target_pairs={{0,64},{8,72},{16,80},{24,88},{32,96},{40,104},{48,112},{56,120},{... | collective-permute-start | bytes 442376 | tf_op jit(solution)/shard_map/ppermute | solution.py:44
  89.5 10.8 %collective-permute-start.7 = (f32[9,1024]{1,0:T(8,128)S(1)}, f32[9,1024]{1,0:T(8,128)S(1)}, u32[]{:S(2)}, u32[]{:S(2)}) collective-permute-start(f32[9,1024]{1,0:T(8,128)S(1)} %get-tuple-element.20), channel_id=1, source_target_pairs={{0,2},{1,3},{2,4},{3,5},{4,6},{5,7},{6,0},{7,1},{8,10},{9,11},{10,... | collective-permute-start | bytes 110600 | tf_op jit(solution)/shard_map/ppermute | solution.py:44
  91.0 9.3 %collective-permute-start.9 = (f32[9,1024]{1,0:T(8,128)S(1)}, f32[9,1024]{1,0:T(8,128)S(1)}, u32[]{:S(2)}, u32[]{:S(2)}) collective-permute-start(f32[9,1024]{1,0:T(8,128)S(1)} %get-tuple-element.21), channel_id=1, source_target_pairs={{0,6},{1,7},{2,0},{3,1},{4,2},{5,3},{6,4},{7,5},{8,14},{9,15},{10,... | collective-permute-start | bytes 110600 | tf_op jit(solution)/shard_map/ppermute | solution.py:44
  92.6 7.8 %collective-permute-start.8 = (f32[9,1024]{1,0:T(8,128)S(1)}, f32[9,1024]{1,0:T(8,128)S(1)}, u32[]{:S(2)}, u32[]{:S(2)}) collective-permute-start(f32[9,1024]{1,0:T(8,128)S(1)} %get-tuple-element.22), channel_id=1, source_target_pairs={{0,4},{1,5},{2,6},{3,7},{4,0},{5,1},{6,2},{7,3},{8,12},{9,13},{10,... | collective-permute-start | bytes 110600 | tf_op jit(solution)/shard_map/ppermute | solution.py:44
  94.6 10.4 %all-to-all-start = ((s32[8,2,512]{2,1,0:T(2,128)}), s32[8,2,512]{2,1,0:T(2,128)S(1)}, u32[]{:S(2)}, u32[]{:S(2)}) async-start(s32[8,2,512]{2,1,0:T(2,128)} %pad_add_fusion), calls=%async_computation | async-start | bytes 65536 | tf_op jit(solution)/shard_map/all_to_all | solution.py:119
  100.4 7.5 %collective-permute-start.10 = (f32[9,1024]{1,0:T(8,128)S(1)}, f32[9,1024]{1,0:T(8,128)S(1)}, u32[]{:S(2)}, u32[]{:S(2)}) collective-permute-start(f32[9,1024]{1,0:T(8,128)S(1)} %get-tuple-element.11), channel_id=1, source_target_pairs={{0,2},{1,3},{2,4},{3,5},{4,6},{5,7},{6,0},{7,1},{8,10},{9,11},{10,... | collective-permute-start | bytes 110600 | tf_op jit(solution)/shard_map/ppermute | solution.py:60
  105.1 4.7 %collective-permute-start.11 = (f32[9,1024]{1,0:T(8,128)S(1)}, f32[9,1024]{1,0:T(8,128)S(1)}, u32[]{:S(2)}, u32[]{:S(2)}) collective-permute-start(f32[9,1024]{1,0:T(8,128)S(1)} %get-tuple-element.11), channel_id=1, source_target_pairs={{0,4},{1,5},{2,6},{3,7},{4,0},{5,1},{6,2},{7,3},{8,12},{9,13},{10,... | collective-permute-start | bytes 110600 | tf_op jit(solution)/shard_map/ppermute | solution.py:60
  106.0 3.8 %collective-permute-start.12 = (f32[9,1024]{1,0:T(8,128)S(1)}, f32[9,1024]{1,0:T(8,128)S(1)}, u32[]{:S(2)}, u32[]{:S(2)}) collective-permute-start(f32[9,1024]{1,0:T(8,128)S(1)} %get-tuple-element.11), channel_id=1, source_target_pairs={{0,6},{1,7},{2,0},{3,1},{4,2},{5,3},{6,4},{7,5},{8,14},{9,15},{10,... | collective-permute-start | bytes 110600 | tf_op jit(solution)/shard_map/ppermute | solution.py:60
  109.8 7.0 %collective-permute-start.13 = (f32[36,1024]{1,0:T(8,128)S(1)}, f32[36,1024]{1,0:T(8,128)S(1)}, u32[]{:S(2)}, u32[]{:S(2)}) collective-permute-start(f32[36,1024]{1,0:T(8,128)S(1)} %reshape.104), channel_id=1, source_target_pairs={{0,32},{8,40},{16,48},{24,56},{32,64},{40,72},{48,80},{56,88},{64,... | collective-permute-start | bytes 442376 | tf_op jit(solution)/shard_map/ppermute | solution.py:60
  114.6 7.7 %collective-permute-start.15 = (f32[36,1024]{1,0:T(8,128)S(1)}, f32[36,1024]{1,0:T(8,128)S(1)}, u32[]{:S(2)}, u32[]{:S(2)}) collective-permute-start(f32[36,1024]{1,0:T(8,128)S(1)} %reshape.104), channel_id=1, source_target_pairs={{0,96},{8,104},{16,112},{24,120},{32,0},{40,8},{48,16},{56,24},{64... | collective-permute-start | bytes 442376 | tf_op jit(solution)/shard_map/ppermute | solution.py:60
  116.6 5.7 %collective-permute-start.14 = (f32[36,1024]{1,0:T(8,128)S(1)}, f32[36,1024]{1,0:T(8,128)S(1)}, u32[]{:S(2)}, u32[]{:S(2)}) collective-permute-start(f32[36,1024]{1,0:T(8,128)S(1)} %reshape.104), channel_id=1, source_target_pairs={{0,64},{8,72},{16,80},{24,88},{32,96},{40,104},{48,112},{56,120},{... | collective-permute-start | bytes 442376 | tf_op jit(solution)/shard_map/ppermute | solution.py:60
  123.2 31.6 %collective-permute-start.17 = (f32[144,1024]{1,0:T(8,128)}, f32[144,1024]{1,0:T(8,128)}, u32[]{:S(2)}, u32[]{:S(2)}) collective-permute-start(f32[144,1024]{1,0:T(8,128)} %reshape.105), channel_id=1, source_target_pairs={{0,16},{8,24},{16,0},{24,8},{32,48},{40,56},{48,32},{56,40},{64,80... | collective-permute-start | bytes 1769480 | tf_op jit(solution)/shard_map/ppermute | solution.py:60
  124.3 28.6 %collective-permute-start.16 = (f32[144,1024]{1,0:T(8,128)}, f32[144,1024]{1,0:T(8,128)}, u32[]{:S(2)}, u32[]{:S(2)}) collective-permute-start(f32[144,1024]{1,0:T(8,128)} %reshape.105), channel_id=1, source_target_pairs={{0,8},{8,16},{16,24},{24,0},{32,40},{40,48},{48,56},{56,32},{64,72... | collective-permute-start | bytes 1769480 | tf_op jit(solution)/shard_map/ppermute | solution.py:60
  135.1 21.7 %collective-permute-start.18 = (f32[144,1024]{1,0:T(8,128)}, f32[144,1024]{1,0:T(8,128)S(1)}, u32[]{:S(2)}, u32[]{:S(2)}) collective-permute-start(f32[144,1024]{1,0:T(8,128)} %reshape.105), channel_id=1, source_target_pairs={{0,24},{8,0},{16,8},{24,16},{32,56},{40,32},{48,40},{56,48},{64,88... | collective-permute-start | bytes 1769480 | tf_op jit(solution)/shard_map/ppermute | solution.py:60
  174.5 4.9 %collective-permute-start.19 = (f32[576,1024]{1,0:T(8,128)}, f32[576,1024]{1,0:T(8,128)S(1)}, u32[]{:S(2)}, u32[]{:S(2)}) collective-permute-start(f32[576,1024]{1,0:T(8,128)} %bitcast.35), channel_id=1, source_target_pairs={{0,1},{1,0},{2,3},{3,2},{4,5},{5,4},{6,7},{7,6},{8,9},{9,8},{10,11... | collective-permute-start | bytes 7077896 | tf_op jit(solution)/shard_map/ppermute | solution.py:53
  175.6 4.1 %copy-start.3 = (f32[1024,1024]{1,0:T(8,128)S(1)}, f32[1024,1024]{1,0:T(8,128)}, u32[]{:S(2)}) copy-start(f32[1024,1024]{1,0:T(8,128)} %param.7) | copy-start | bytes 12582916
  181.6 2.0 copy-start.4
Sparse Core Ops, SparseCore 0:
  9.7 90.2 all-gather.2
